TPU v7x, 32 devices: a whole 2x2x4 slice. The times are simulated.
32 devices in a mesh: row: 8 (over z, core), col: 4 (over y, x).
Axes of the slice: x: 2, y: 2, z: 4, core: 2. Of those that a mesh axis runs over, the one named last changes fastest.
Arguments:
- demand: float32 [2048, 4096], P('row', 'col'), may hold values from 0.2 to 2
- leakage: float32 [2048, 4096], P('row', 'col'), may hold values from 0.05 to 0.5
- conductance: float32 [2048, 4096], P('row', 'col'), may hold values from 0.5 to 4
- vias: int32 [2048, 4096], P('row', 'col'), may hold values 0 or 1
- layer_of: int32 [256, 512], P('row'), may hold values from 0 to 31
- lateral_k: float32 [32, 256, 512], P('col', 'row'), may hold values from 0.3 to 3
- vertical_k: float32 [32, 256, 512], P('col', 'row'), may hold values from 0.1 to 1
Outputs:
- drop: float32 [2048, 4096], P('row', 'col')
- temperature: float32 [32, 256, 512], P('col', 'row')
All inputs are finite; a program needn't handle non-finite values. No bound on the sum of `vias` on one device may be relied on, other than what follows from the above.
Results may differ from a plain program's by a relative error of at most 0.0001.
Values sent between devices are 32-bit elements; how exact they have to be, the bound alone decides.
No kernel may reach another device: no remote copies, remote signals or barrier semaphores. Data moves between devices by JAX's collectives and lax.ppermute only.
A program may use at most 128 MiB of HBM per device.

v0:
```python
import os

import jax
import jax.numpy as jnp
from jax import lax
from jax.experimental import pallas as pl
from jax.experimental.pallas import tpu as pltpu
from jax.sharding import PartitionSpec as P

INTERPRET = os.environ.get("SOL_INTERPRET") == "1"

COARSE = 8
SWEEPS = 4
HEAT_SWEEPS = 4
OUTER = 2


COND_SLOPE = 0.5
LEAK_SLOPE = 0.7
VIA_CONDUCT = 4.0

HALO = 4


def extended(block, sides):
    for axis, dim, width in sides:
        count = lax.axis_size(axis)
        forward = [(i, i + 1) for i in range(count - 1)]
        backward = [(target, source) for source, target in forward]
        low = lax.ppermute(
            lax.slice_in_dim(block, block.shape[dim] - width, None, axis=dim), axis, forward
        )
        high = lax.ppermute(lax.slice_in_dim(block, 0, width, axis=dim), axis, backward)
        block = jnp.concatenate([low, block, high], axis=dim)
    return block


def spread_cols(coarse, fine_cols):
    n = coarse.shape[1]
    ids = jnp.arange(fine_cols, dtype=jnp.int32) // COARSE
    onehot = (jnp.arange(n, dtype=jnp.int32)[:, None] == ids[None, :]).astype(jnp.float32)
    return jnp.dot(coarse, onehot, precision=lax.Precision.HIGHEST)


def fine_of(coarse, fine_cols):
    wide = spread_cols(coarse, fine_cols)
    rows = wide.shape[0]
    return jnp.broadcast_to(wide[:, None, :], (rows, COARSE, fine_cols)).reshape(rows * COARSE, fine_cols)


def coarse_of(fine):
    rows, cols = fine.shape
    summed_rows = jnp.sum(fine.reshape(rows // COARSE, COARSE, cols), axis=1)
    n = cols // COARSE
    ids = jnp.arange(cols, dtype=jnp.int32) // COARSE
    onehot = (ids[:, None] == jnp.arange(n, dtype=jnp.int32)[None, :]).astype(jnp.float32)
    return jnp.dot(summed_rows, onehot, precision=lax.Precision.HIGHEST) * (1.0 / (COARSE * COARSE))


def row_above(x, above):
    sub = lax.broadcasted_iota(jnp.int32, x.shape, 0)
    return jnp.where(sub == 0, pltpu.roll(above, 1, 0), pltpu.roll(x, 1, 0))


def row_below(x, below):
    n = x.shape[0]
    sub = lax.broadcasted_iota(jnp.int32, x.shape, 0)
    return jnp.where(sub == n - 1, pltpu.roll(below, n - 1, 0), pltpu.roll(x, n - 1, 0))


def rows_of(k):
    return pl.ds(pl.multiple_of(k * 8, 8), 8)


def chunk(ref, k, count):
    return ref[rows_of(jnp.clip(k, 0, count - 1)), :]


def power_kernel(d_ref, c_ref, l_ref, v_ref, rok_ref, cok_ref, o_ref, wn_ref, ws_ref, ww_ref, we_ref, den_ref, buf_ref):
    n, w = c_ref.shape
    count = n // 8

    def weights(k, carry):
        sl = rows_of(k)
        x = c_ref[sl, :]
        a = (x + row_above(x, chunk(c_ref, k - 1, count))) * 0.5
        b = (x + row_below(x, chunk(c_ref, k + 1, count))) * 0.5
        e = (x + pltpu.roll(x, 1, 1)) * 0.5
        f = (x + pltpu.roll(x, w - 1, 1)) * 0.5
        wn_ref[sl, :] = a
        ws_ref[sl, :] = b
        ww_ref[sl, :] = e
        we_ref[sl, :] = f
        den_ref[sl, :] = a + b + e + f + v_ref[sl, :]
        return carry

    lax.fori_loop(0, count, weights, 0)
    col_ok = cok_ref[...] > 0.5

    def sweep(src, dst):
        def body(k, carry):
            sl = rows_of(k)
            x = src[sl, :]
            summed = (
                l_ref[sl, :]
                + wn_ref[sl, :] * row_above(x, chunk(src, k - 1, count))
                + ws_ref[sl, :] * row_below(x, chunk(src, k + 1, count))
                + ww_ref[sl, :] * pltpu.roll(x, 1, 1)
                + we_ref[sl, :] * pltpu.roll(x, w - 1, 1)
            )
            ok = (rok_ref[sl, :] > 0.5) & col_ok
            dst[sl, :] = jnp.where(ok, summed / den_ref[sl, :], 0.0)
            return carry

        lax.fori_loop(0, count, body, 0)

    sweep(d_ref, buf_ref)
    sweep(buf_ref, o_ref)
    sweep(o_ref, buf_ref)
    sweep(buf_ref, o_ref)


def run_power(drop, cond, load, via, row_ok, col_ok):
    n, w = cond.shape
    return pl.pallas_call(
        power_kernel,
        out_shape=jax.ShapeDtypeStruct((n, w), jnp.float32),
        scratch_shapes=[pltpu.VMEM((n, w), jnp.float32) for _ in range(6)],
        compiler_params=pltpu.CompilerParams(vmem_limit_bytes=60 * 1024 * 1024),
        interpret=INTERPRET,
    )(drop, cond, load, via, row_ok, col_ok)


def thermal_kernel(t_ref, s_ref, lk_ref, vk_ref, rok_ref, o_ref, wb_ref, wa_ref, den_ref, buf_ref, *, stride):
    n, w = lk_ref.shape
    count = n // 8
    lane = lax.broadcasted_iota(jnp.int32, (8, w), 1)
    first = lane == 0
    last = lane == w - 1

    def lateral(x, k, ref):
        up = row_above(x, chunk(ref, k - 1, count))
        dn = row_below(x, chunk(ref, k + 1, count))
        lf = jnp.where(first, 0.0, pltpu.roll(x, 1, 1))
        rt = jnp.where(last, 0.0, pltpu.roll(x, w - 1, 1))
        return up, dn, lf, rt

    def weights(k, carry):
        sl = rows_of(k)
        x = lk_ref[sl, :]
        up, dn, lf, rt = lateral(x, k, lk_ref)
        v = vk_ref[sl, :]
        b = (v + chunk(vk_ref, k - stride, count)) * 0.5
        a = (v + chunk(vk_ref, k + stride, count)) * 0.5
        wb_ref[sl, :] = b
        wa_ref[sl, :] = a
        den_ref[sl, :] = (x + up) * 0.5 + (x + dn) * 0.5 + (x + lf) * 0.5 + (x + rt) * 0.5 + b + a
        return carry

    lax.fori_loop(0, count, weights, 0)

    def sweep(src, dst):
        def body(k, carry):
            sl = rows_of(k)
            lk = lk_ref[sl, :]
            kup, kdn, klf, krt = lateral(lk, k, lk_ref)
            x = src[sl, :]
            up, dn, lf, rt = lateral(x, k, src)
            summed = (
                s_ref[sl, :]
                + (lk + kup) * 0.5 * up
                + (lk + kdn) * 0.5 * dn
                + (lk + klf) * 0.5 * lf
                + (lk + krt) * 0.5 * rt
                + wb_ref[sl, :] * chunk(src, k - stride, count)
                + wa_ref[sl, :] * chunk(src, k + stride, count)
            )
            dst[sl, :] = jnp.where(rok_ref[sl, :] > 0.5, summed / den_ref[sl, :], 0.0)
            return carry

        lax.fori_loop(0, count, body, 0)

    sweep(t_ref, buf_ref)
    sweep(buf_ref, o_ref)
    sweep(o_ref, buf_ref)
    sweep(buf_ref, o_ref)


def run_thermal(temp, source, lat, vert, row_ok, stride):
    n, w = lat.shape
    return pl.pallas_call(
        lambda *refs: thermal_kernel(*refs, stride=stride),
        out_shape=jax.ShapeDtypeStruct((n, w), jnp.float32),
        scratch_shapes=[pltpu.VMEM((n, w), jnp.float32) for _ in range(4)],
        compiler_params=pltpu.CompilerParams(vmem_limit_bytes=60 * 1024 * 1024),
        interpret=INTERPRET,
    )(temp, source, lat, vert, row_ok)


def inside_of(start, count, total):
    idx = start + jnp.arange(count, dtype=jnp.int32)
    return (idx >= 0) & (idx < total)


def body(demand, leakage, conductance, vias, layer_of, lateral_k, vertical_k):
    tile_rows, tile_cols = demand.shape
    group_layers, cell_rows, therm_cols = lateral_k.shape
    cell_cols = tile_cols // COARSE
    n_r = lax.axis_size("row")
    n_c = lax.axis_size("col")
    r_idx = lax.axis_index("row")
    c_idx = lax.axis_index("col")
    all_layers = group_layers * n_c
    all_rows = cell_rows * n_r
    total_rows = tile_rows * n_r
    total_cols = tile_cols * n_c

    T0 = 2 * HEAT_SWEEPS
    T1 = HEAT_SWEEPS
    H0 = T0 - 1
    H1 = T1 - 1
    S = SWEEPS
    R1 = H1 * COARSE + SWEEPS
    R0 = max(H0 * COARSE, R1) + SWEEPS
    CW = 64
    PR = -(-R1 // COARSE)
    PC = CW // COARSE

    via_g = VIA_CONDUCT * vias.astype(jnp.float32)
    load0 = demand + leakage

    p0 = extended(jnp.stack([conductance, load0, via_g]), (("row", 1, R0), ("col", 2, CW)))
    p1 = extended(jnp.stack([demand, leakage]), (("row", 1, R1), ("col", 2, CW)))
    k_ext = extended(jnp.stack([lateral_k, vertical_k]), (("row", 2, T0), ("col", 1, T0)))
    layer_ext = extended(layer_of, (("row", 0, T0),))

    cols_w = tile_cols + 2 * CW
    col_ok = inside_of(c_idx * tile_cols - CW, cols_w, total_cols).astype(jnp.float32)[None, :]

    rows0 = tile_rows + 2 * R0
    row_ok0 = inside_of(r_idx * tile_rows - R0, rows0, total_rows).astype(jnp.float32)[:, None]
    drop0 = run_power(jnp.zeros((rows0, cols_w), jnp.float32), p0[0], p0[1], p0[2], row_ok0, col_ok)
    hr0 = H0 * COARSE
    rs = slice(R0 - hr0, R0 + tile_rows + hr0)
    cs = slice(CW, CW + tile_cols)
    d_h = drop0[rs, cs]
    heat0 = coarse_of(p0[1][rs, cs] * (1.0 - d_h) + p0[0][rs, cs] * d_h * d_h)

    def gather_heat(heat):
        copies = jnp.broadcast_to(heat[None], (n_c,) + heat.shape)
        gathered = lax.all_to_all(copies, "col", split_axis=0, concat_axis=0, tiled=True)
        gathered = gathered.transpose(1, 0, 2).reshape(heat.shape[0], n_c * cell_cols)
        return jnp.pad(gathered, ((1, 1), (0, 0)))

    def thermal(temp_ext, heat_ext, halo):
        layers = group_layers + 2 * halo
        rows = cell_rows + 2 * halo
        ks = k_ext[:, T0 - halo:T0 + group_layers + halo, T0 - halo:T0 + cell_rows + halo]
        tlay = c_idx * group_layers - halo + jnp.arange(layers, dtype=jnp.int32)
        inside = inside_of(c_idx * group_layers - halo, layers, all_layers)[:, None] & inside_of(r_idx * cell_rows - halo, rows, all_rows)[None, :]
        lay_in = layer_ext[T0 - halo:T0 + cell_rows + halo]
        picker = (lay_in[None, :, :] == tlay[:, None, None]) & inside[:, :, None]
        source = jnp.where(picker, heat_ext[None, :, :], 0.0)
        flat = (layers * rows, therm_cols)
        out = run_thermal(
            temp_ext.reshape(flat), source.reshape(flat), ks[0].reshape(flat), ks[1].reshape(flat),
            inside.astype(jnp.float32).reshape(layers * rows, 1), rows // 8,
        )
        return out.reshape(layers, rows, therm_cols)

    temp0 = thermal(jnp.zeros((group_layers + 2 * T0, cell_rows + 2 * T0, therm_cols), jnp.float32), gather_heat(heat0), T0)
    temp0 = temp0[T0 - T1:T0 + group_layers + T1, T0 - T1:T0 + cell_rows + T1]

    own_layers = c_idx * group_layers + jnp.arange(group_layers, dtype=jnp.int32)
    t_own = temp0[T1:T1 + group_layers, T1 - PR:T1 + cell_rows + PR]
    lay_w = layer_ext[T0 - PR:T0 + cell_rows + PR]
    partial = jnp.sum(jnp.where(lay_w[None, :, :] == own_layers[:, None, None], t_own, 0.0), axis=0)
    partial = jnp.pad(partial, ((0, 0), (PC, PC)))
    windows = jnp.stack([partial[:, j * cell_cols:j * cell_cols + cell_cols + 2 * PC] for j in range(n_c)])
    windows = lax.all_to_all(windows, "col", split_axis=0, concat_axis=0, tiled=True)
    cell_temp = jnp.sum(windows, axis=0)

    denom_c = 1.0 + COND_SLOPE * cell_temp
    grow_c = jnp.exp(LEAK_SLOPE * cell_temp)
    rows1 = tile_rows + 2 * R1
    fo = PR * COARSE - R1
    denom_f = fine_of(denom_c, cols_w)[fo:fo + rows1]
    grow_f = fine_of(grow_c, cols_w)[fo:fo + rows1]
    rs1 = slice(R0 - R1, R0 - R1 + rows1)
    cond1 = p0[0][rs1] / denom_f
    load1 = p1[0] + p1[1] * grow_f
    row_ok1 = inside_of(r_idx * tile_rows - R1, rows1, total_rows).astype(jnp.float32)[:, None]
    drop1 = run_power(drop0[rs1], cond1, load1, p0[2][rs1], row_ok1, col_ok)
    hr1 = H1 * COARSE
    rh = slice(R1 - hr1, R1 + tile_rows + hr1)
    d_h1 = drop1[rh, cs]
    heat1 = coarse_of(load1[rh, cs] * (1.0 - d_h1) + cond1[rh, cs] * d_h1 * d_h1)
    temp1 = thermal(temp0, gather_heat(heat1), T1)
    temp_out = temp1[T1:T1 + group_layers, T1:T1 + cell_rows]
    drop_out = drop1[R1:R1 + tile_rows, cs]
    return (drop_out, temp_out)


def solution(mesh):
    in_specs = (
        P("row", "col"),
        P("row", "col"),
        P("row", "col"),
        P("row", "col"),
        P("row", None),
        P("col", "row", None),
        P("col", "row", None),
    )
    out_specs = (P("row", "col"), P("col", "row", None))
    return jax.shard_map(body, mesh=mesh, in_specs=in_specs, out_specs=out_specs, check_vma=False)
```

profile of v0, /device:TPU:8, one launch (start us, length us, event | category | flops | bytes accessed | tf_op | source)
XLA Modules:
  0.0 325.8 jit_solution(515161685866688240)
XLA Ops:
  0.7 1.5 multiply_bitcast_fusion
  2.7 0.8 copy-done.14
  3.5 1.0 copy-done.20
  4.5 1.3 pad_maximum_fusion.6
  5.8 2.1 collective-permute-start.1
  7.9 2.4 collective-permute-start
  10.9 3.1 collective-permute-start.4
  14.1 2.5 collective-permute-start.11
  16.5 1.9 collective-permute-start.10
  19.1 0.7 fusion.19.rok_ref
  19.8 0.7 fusion.23.rok_ref
  20.5 0.8 pad_maximum_fusion.10
  22.5 1.1 reshape.293.refs_4_
  24.1 0.9 reshape.294.refs_4_
  26.2 3.6 %collective-permute-start.5 = (s32[8,512]{1,0:T(8,128)}, s32[8,512]{1,0:T(8,128)S(1)}, u32[]{:S(2)}, u32[]{:S(2)}) collective-permute-start(s32[8,512]{1,0:T(8,128)} %get-tuple-element.23), channel_id=1, source_target_pairs={{4,0},{8,4},{12,8},{16,12},{20,16},{24,20},{28,24},{5,1},{9,5},{13... | collective-permute-start | bytes 49160 | tf_op jit(solution)/shard_map/ppermute | solution.py:33
  29.9 1.9 collective-permute-start.7
  31.8 0.7 copy-done.25
  32.5 2.7 collective-permute-start.6
  35.2 2.0 pad_maximum_fusion.2
  37.2 2.8 pad_maximum_fusion.1
  40.0 2.1 copy-done.1
  42.1 1.2 fusion.44
  43.3 2.0 copy.33
  45.3 4.1 %collective-permute-start.2 = (f32[3,376,64]{1,2,0:T(8,128)}, f32[3,376,64]{1,2,0:T(8,128)}, u32[]{:S(2)}, u32[]{:S(2)}) collective-permute-start(f32[3,376,64]{1,2,0:T(8,128)} %copy.33), channel_id=1, source_target_pairs={{0,1},{1,2},{2,3},{4,5},{5,6},{6,7},{8,9},{9,10},{10,11},{12,13},{... | collective-permute-start | bytes 866312 | tf_op jit(solution)/shard_map/ppermute | solution.py:30
  49.5 2.0 copy.34
  51.4 1.3 collective-permute-start.3
  52.8 2.5 pad_maximum_fusion.3
  55.3 1.3 collective-permute-start.9
  56.6 6.3 %collective-permute-start.8 = (f32[2,8,48,512]{3,2,1,0:T(8,128)}, f32[2,8,48,512]{3,2,1,0:T(8,128)}, u32[]{:S(2)}, u32[]{:S(2)}) collective-permute-start(f32[2,8,48,512]{3,2,1,0:T(8,128)} %pad_maximum_fusion.3), channel_id=1, source_target_pairs={{0,1},{1,2},{2,3},{4,5},{5,6},{6,7},{8,9},{9,10},{10,11},{12,13},{... | collective-permute-start | bytes 4718600 | tf_op jit(solution)/shard_map/ppermute | solution.py:30
  62.9 0.9 fusion.45
  63.9 4.4 %collective-permute-start.12 = (f32[2,312,64]{2,1,0:T(8,128)}, f32[2,312,64]{2,1,0:T(8,128)}, u32[]{:S(2)}, u32[]{:S(2)}) collective-permute-start(f32[2,312,64]{2,1,0:T(8,128)} %get-tuple-element.14), channel_id=1, source_target_pairs={{0,1},{1,2},{2,3},{4,5},{5,6},{6,7},{8,9},{9,10},{10,11},{12,13},{... | collective-permute-start | bytes 479240 | tf_op jit(solution)/shard_map/ppermute | solution.py:30
  68.3 1.2 copy.35
  69.5 1.3 collective-permute-start.13
  70.8 1.2 copy.36
  72.0 6.9 %concatenate.22 = f32[3,376,1152]{2,1,0:T(8,128)} concatenate(f32[3,376,64]{2,1,0:T(8,128)S(1)} %copy.35, f32[3,376,1024]{2,1,0:T(8,128)} %copy-done.1, f32[3,376,64]{2,1,0:T(8,128)S(1)} %copy.36), dimensions={2} | concatenate | bytes 10395648 | tf_op jit(solution)/shard_map/concatenate | solution.py:34
  78.9 4.9 %slice_bitcast_fusion = (f32[376,1152]{1,0:T(8,128)}, f32[376,1152]{1,0:T(8,128)}, f32[376,1152]{1,0:T(8,128)}) fusion(f32[3,376,1152]{2,1,0:T(8,128)} %concatenate.22), kind=kLoop, calls=%fused_computation.8 | loop fusion | bytes 10395648 | tf_op jit(solution)/shard_map/squeeze | solution.py:242
  83.8 1.3 broadcast_in_dim.36.d_ref
  85.2 26.9 %shard_map.86 = f32[376,1152]{1,0:T(8,128)} custom-call(f32[376,1152]{1,0:T(8,128)} %broadcast_in_dim.36.d_ref, f32[376,1152]{1,0:T(8,128)} %get-tuple-element.4.c_ref, f32[376,1152]{1,0:T(8,128)} %get-tuple-element.3.l_ref, f32[376,1152]{1,0:T(8,128)} %get-tuple-element.2.v_ref, f32[376,1]{1,0:T(8,128)} %fusion.19.rok_ref, f32[1,1152]{1,0:T(1,128)} %and_convert_fusion.cok_ref), custom_call_target="tpu_custom_call" | custom-call | tf_op jit(solution)/shard_map/pallas_call | solution.py:125
  112.1 2.9 fusion.3
  116.1 4.5 %all-to-all-start = ((f32[4,46,128]{2,1,0:T(8,128)}), f32[4,46,128]{2,1,0:T(8,128)S(1)}, u32[]{:S(2)}, u32[]{:S(2)}) async-start(f32[4,46,128]{2,1,0:T(8,128)} %broadcast_in_dim.37), calls=%async_computation | async-start | bytes 196608 | tf_op jit(solution)/shard_map/all_to_all | solution.py:251
  120.6 25.0 %collective-permute-done.13 = f32[2,312,64]{2,1,0:T(8,128)} collective-permute-done((f32[2,312,64]{2,1,0:T(8,128)}, f32[2,312,64]{2,1,0:T(8,128)}, u32[]{:S(2)}, u32[]{:S(2)}) %collective-permute-start.13) | collective-permute-done | bytes 159776 | tf_op jit(solution)/shard_map/ppermute | solution.py:33
  145.6 4.7 %concatenate.27 = f32[2,312,1152]{2,1,0:T(8,128)} concatenate(f32[2,312,64]{2,1,0:T(8,128)} %collective-permute-done.12, f32[2,312,1024]{2,1,0:T(8,128)} %copy-done.4, f32[2,312,64]{2,1,0:T(8,128)} %collective-permute-done.13), dimensions={2} | concatenate | bytes 5750784 | tf_op jit(solution)/shard_map/concatenate | solution.py:34
  150.5 2.1 bitcast_select_fusion.refs_1_
  152.6 2.3 pad_maximum_fusion
  154.9 3.5 %fusion.43 = (f32[1,24,48,512]{3,2,1,0:T(8,128)}, f32[1,24,48,512]{3,2,1,0:T(8,128)}) fusion(f32[2,24,48,512]{3,2,1,0:T(8,128)S(1)} %pad_maximum_fusion), kind=kLoop, calls=%fused_computation.108 | loop fusion | bytes 9437184 | tf_op jit(solution)/shard_map/slice | solution.py:266
  158.5 1.7 reshape.281.refs_0_
  160.2 69.7 %shard_map.87 = f32[1152,512]{1,0:T(8,128)} custom-call(f32[1152,512]{1,0:T(8,128)} %reshape.281.refs_0_, f32[1152,512]{1,0:T(8,128)} %bitcast_select_fusion.refs_1_, f32[1152,512]{1,0:T(8,128)} %bitcast.91, f32[1152,512]{1,0:T(8,128)} %bitcast.90, f32[1152,1]{1,0:T(8,128)} %reshape.293.refs_4_), custom_call_target="tpu_custom_call" | custom-call | tf_op jit(solution)/shard_map/pallas_call | solution.py:191
  229.9 1.3 fusion.11
  231.4 0.7 pad_maximum_fusion.11
  232.1 3.7 %all-to-all-start.1 = ((f32[4,40,144]{2,1,0:T(8,128)}), f32[4,40,144]{2,1,0:T(8,128)S(1)}, u32[]{:S(2)}, u32[]{:S(2)}) async-start(f32[4,40,144]{2,1,0:T(8,128)} %pad_maximum_fusion.11), calls=%async_computation.1 | async-start | bytes 327680 | tf_op jit(solution)/shard_map/all_to_all | solution.py:280
  235.7 2.5 slice_bitcast_fusion.3.v_ref
  238.3 1.3 slice.190.d_ref
  239.5 1.3 all-to-all-done.1
  241.6 2.9 slice_divide_fusion.c_ref
  244.6 1.5 fusion.4.l_ref
  246.1 22.6 %shard_map.88 = f32[312,1152]{1,0:T(8,128)} custom-call(f32[312,1152]{1,0:T(8,128)} %slice.190.d_ref, f32[312,1152]{1,0:T(8,128)} %slice_divide_fusion.c_ref, f32[312,1152]{1,0:T(8,128)} %fusion.4.l_ref, f32[312,1152]{1,0:T(8,128)} %slice_bitcast_fusion.3.v_ref, f32[312,1]{1,0:T(8,128)} %fusion.23.rok_ref, f32[1,1152]{1,0:T(1,128)} %and_convert_fusion.cok_ref), custom_call_target="tpu_custom_call" | custom-call | tf_op jit(solution)/shard_map/pallas_call | solution.py:125
  268.7 2.5 fusion.8
  272.3 3.3 %all-to-all-start.2 = ((f32[4,38,128]{2,1,0:T(8,128)}), f32[4,38,128]{2,1,0:T(8,128)S(1)}, u32[]{:S(2)}, u32[]{:S(2)}) async-start(f32[4,38,128]{2,1,0:T(8,128)} %broadcast_in_dim.43), calls=%async_computation.2 | async-start | bytes 163840 | tf_op jit(solution)/shard_map/all_to_all | solution.py:251
  275.6 4.1 %fusion.42 = (f32[1,16,40,512]{3,2,1,0:T(8,128)}, f32[1,16,40,512]{3,2,1,0:T(8,128)}) fusion(f32[2,24,48,512]{3,2,1,0:T(8,128)} %copy-done), kind=kLoop, calls=%fused_computation.107 | loop fusion | bytes 5242880 | tf_op jit(solution)/shard_map/slice | solution.py:266
  279.7 1.2 slice.209
  281.5 1.3 slice.208
  283.0 1.4 bitcast_select_fusion.1.refs_1_
  284.4 39.5 %shard_map.89 = f32[640,512]{1,0:T(8,128)} custom-call(f32[640,512]{1,0:T(8,128)} %bitcast.96, f32[640,512]{1,0:T(8,128)} %bitcast_select_fusion.1.refs_1_, f32[640,512]{1,0:T(8,128)} %bitcast.95, f32[640,512]{1,0:T(8,128)} %bitcast.94, f32[640,1]{1,0:T(8,128)} %reshape.294.refs_4_), custom_call_target="tpu_custom_call" | custom-call | tf_op jit(solution)/shard_map/pallas_call | solution.py:191
  323.9 1.9 slice.215
  (122 shorter events, 8.7 us)
Async XLA Ops:
  0.6 1.5 copy-start.10
  0.6 1.8 copy-start.11
  2.5 1.0 copy-start.14
  2.5 2.0 copy-start.20
  2.7 3.1 copy-start.12
  4.5 5.8 %copy-start.26 = (s32[32,512]{1,0:T(8,128)S(1)}, s32[32,512]{1,0:T(8,128)}, u32[]{:S(2)}) copy-start(s32[32,512]{1,0:T(8,128)} %param.11) | copy-start | bytes 196612
  5.8 14.7 %copy-start.17 = (f32[8,32,512]{2,1,0:T(8,128)S(1)}, f32[8,32,512]{2,1,0:T(8,128)}, u32[]{:S(2)}) copy-start(f32[8,32,512]{2,1,0:T(8,128)} %param.13) | copy-start | bytes 1572868
  5.8 14.7 %copy-start.18 = (f32[8,32,512]{2,1,0:T(8,128)S(1)}, f32[8,32,512]{2,1,0:T(8,128)}, u32[]{:S(2)}) copy-start(f32[8,32,512]{2,1,0:T(8,128)} %param.12) | copy-start | bytes 1572868
  5.8 31.3 %collective-permute-start.1 = (f32[3,60,1024]{2,1,0:T(8,128)}, f32[3,60,1024]{2,1,0:T(8,128)}, u32[]{:S(2)}, u32[]{:S(2)}) collective-permute-start(f32[3,60,1024]{2,1,0:T(8,128)} %get-tuple-element.12), channel_id=1, source_target_pairs={{4,0},{8,4},{12,8},{16,12},{20,16},{24,20},{28,24},{5,1},{9,5},{13... | collective-permute-start | bytes 2211848 | tf_op jit(solution)/shard_map/ppermute | solution.py:33
  7.9 29.3 %collective-permute-start = (f32[3,60,1024]{2,1,0:T(8,128)}, f32[3,60,1024]{2,1,0:T(8,128)}, u32[]{:S(2)}, u32[]{:S(2)}) collective-permute-start(f32[3,60,1024]{2,1,0:T(8,128)} %get-tuple-element.11), channel_id=1, source_target_pairs={{0,4},{4,8},{8,12},{12,16},{16,20},{20,24},{24,28},{1,5},{5,9},{9,... | collective-permute-start | bytes 2211848 | tf_op jit(solution)/shard_map/ppermute | solution.py:30
  10.9 15.3 %collective-permute-start.4 = (s32[8,512]{1,0:T(8,128)S(1)}, s32[8,512]{1,0:T(8,128)S(1)}, u32[]{:S(2)}, u32[]{:S(2)}) collective-permute-start(s32[8,512]{1,0:T(8,128)S(1)} %get-tuple-element.24), channel_id=1, source_target_pairs={{0,4},{4,8},{8,12},{12,16},{16,20},{20,24},{24,28},{1,5},{5,9},{9,... | collective-permute-start | bytes 49160 | tf_op jit(solution)/shard_map/ppermute | solution.py:30
  14.1 15.8 %collective-permute-start.11 = (f32[2,28,1024]{2,1,0:T(8,128)S(1)}, f32[2,28,1024]{2,1,0:T(8,128)S(1)}, u32[]{:S(2)}, u32[]{:S(2)}) collective-permute-start(f32[2,28,1024]{2,1,0:T(8,128)S(1)} %get-tuple-element.16), channel_id=1, source_target_pairs={{4,0},{8,4},{12,8},{16,12},{20,16},{24,20},{28,24},{5,1},{9,5},{13... | collective-permute-start | bytes 688136 | tf_op jit(solution)/shard_map/ppermute | solution.py:33
  16.5 15.3 %collective-permute-start.10 = (f32[2,28,1024]{2,1,0:T(8,128)S(1)}, f32[2,28,1024]{2,1,0:T(8,128)S(1)}, u32[]{:S(2)}, u32[]{:S(2)}) collective-permute-start(f32[2,28,1024]{2,1,0:T(8,128)S(1)} %get-tuple-element.15), channel_id=1, source_target_pairs={{0,4},{4,8},{8,12},{12,16},{16,20},{20,24},{24,28},{1,5},{5,9},{9,... | collective-permute-start | bytes 688136 | tf_op jit(solution)/shard_map/ppermute | solution.py:30
  26.2 94.4 %collective-permute-start.5 = (s32[8,512]{1,0:T(8,128)}, s32[8,512]{1,0:T(8,128)S(1)}, u32[]{:S(2)}, u32[]{:S(2)}) collective-permute-start(s32[8,512]{1,0:T(8,128)} %get-tuple-element.23), channel_id=1, source_target_pairs={{4,0},{8,4},{12,8},{16,12},{20,16},{24,20},{28,24},{5,1},{9,5},{13... | collective-permute-start | bytes 49160 | tf_op jit(solution)/shard_map/ppermute | solution.py:33
  29.8 2.0 copy-start.24
  29.9 22.9 %collective-permute-start.7 = (f32[2,8,8,512]{3,2,1,0:T(8,128)}, f32[2,8,8,512]{3,2,1,0:T(8,128)S(1)}, u32[]{:S(2)}, u32[]{:S(2)}) collective-permute-start(f32[2,8,8,512]{3,2,1,0:T(8,128)} %get-tuple-element.18), channel_id=1, source_target_pairs={{4,0},{8,4},{12,8},{16,12},{20,16},{24,20},{28,24},{5,1},{9,5},{13... | collective-permute-start | bytes 786440 | tf_op jit(solution)/shard_map/ppermute | solution.py:33
  31.8 0.7 copy-start.25
  32.5 4.7 %copy-start.13 = (f32[1,256,1024]{2,1,0:T(8,128)S(1)}, f32[1,256,1024]{2,1,0:T(8,128)}, u32[]{:S(2)}) copy-start(f32[1,256,1024]{2,1,0:T(8,128)} %copy-done.12) | copy-start | bytes 3145732
  32.5 4.7 %copy-start.15 = (f32[1,256,1024]{2,1,0:T(8,128)S(1)}, f32[1,256,1024]{2,1,0:T(8,128)}, u32[]{:S(2)}) copy-start(f32[1,256,1024]{2,1,0:T(8,128)} %copy-done.14) | copy-start | bytes 3145732
  32.5 4.7 %copy-start.21 = (f32[256,1024]{1,0:T(8,128)S(1)}, f32[256,1024]{1,0:T(8,128)}, u32[]{:S(2)}) copy-start(f32[256,1024]{1,0:T(8,128)} %param.9) | copy-start | bytes 3145732
  32.5 20.3 %collective-permute-start.6 = (f32[2,8,8,512]{3,2,1,0:T(8,128)}, f32[2,8,8,512]{3,2,1,0:T(8,128)}, u32[]{:S(2)}, u32[]{:S(2)}) collective-permute-start(f32[2,8,8,512]{3,2,1,0:T(8,128)} %get-tuple-element.17), channel_id=1, source_target_pairs={{0,4},{4,8},{8,12},{12,16},{16,20},{20,24},{24,28},{1,5},{5,9},{9,... | collective-permute-start | bytes 786440 | tf_op jit(solution)/shard_map/ppermute | solution.py:30
  37.1 25.8 %copy-start.4 = (f32[2,312,1024]{2,1,0:T(8,128)}, f32[2,312,1024]{2,1,0:T(8,128)S(1)}, u32[]{:S(2)}) copy-start(f32[2,312,1024]{2,1,0:T(8,128)S(1)} %pad_maximum_fusion.2) | copy-start | bytes 7667716
  40.0 2.2 copy-start.1
  45.3 18.5 %collective-permute-start.2 = (f32[3,376,64]{1,2,0:T(8,128)}, f32[3,376,64]{1,2,0:T(8,128)}, u32[]{:S(2)}, u32[]{:S(2)}) collective-permute-start(f32[3,376,64]{1,2,0:T(8,128)} %copy.33), channel_id=1, source_target_pairs={{0,1},{1,2},{2,3},{4,5},{5,6},{6,7},{8,9},{9,10},{10,11},{12,13},{... | collective-permute-start | bytes 866312 | tf_op jit(solution)/shard_map/ppermute | solution.py:30
  51.4 18.0 %collective-permute-start.3 = (f32[3,376,64]{1,2,0:T(8,128)}, f32[3,376,64]{1,2,0:T(8,128)}, u32[]{:S(2)}, u32[]{:S(2)}) collective-permute-start(f32[3,376,64]{1,2,0:T(8,128)} %copy.34), channel_id=1, source_target_pairs={{1,0},{2,1},{3,2},{5,4},{6,5},{7,6},{9,8},{10,9},{11,10},{13,12},{... | collective-permute-start | bytes 866312 | tf_op jit(solution)/shard_map/ppermute | solution.py:33
  52.7 2.5 copy-start.22
  55.3 97.2 %collective-permute-start.9 = (f32[2,8,48,512]{3,2,1,0:T(8,128)}, f32[2,8,48,512]{3,2,1,0:T(8,128)}, u32[]{:S(2)}, u32[]{:S(2)}) collective-permute-start(f32[2,8,48,512]{3,2,1,0:T(8,128)} %pad_maximum_fusion.3), channel_id=1, source_target_pairs={{1,0},{2,1},{3,2},{5,4},{6,5},{7,6},{9,8},{10,9},{11,10},{13,12},{... | collective-permute-start | bytes 4718600 | tf_op jit(solution)/shard_map/ppermute | solution.py:33
  56.6 96.0 %collective-permute-start.8 = (f32[2,8,48,512]{3,2,1,0:T(8,128)}, f32[2,8,48,512]{3,2,1,0:T(8,128)}, u32[]{:S(2)}, u32[]{:S(2)}) collective-permute-start(f32[2,8,48,512]{3,2,1,0:T(8,128)} %pad_maximum_fusion.3), channel_id=1, source_target_pairs={{0,1},{1,2},{2,3},{4,5},{5,6},{6,7},{8,9},{9,10},{10,11},{12,13},{... | collective-permute-start | bytes 4718600 | tf_op jit(solution)/shard_map/ppermute | solution.py:30
  63.9 56.8 %collective-permute-start.12 = (f32[2,312,64]{2,1,0:T(8,128)}, f32[2,312,64]{2,1,0:T(8,128)}, u32[]{:S(2)}, u32[]{:S(2)}) collective-permute-start(f32[2,312,64]{2,1,0:T(8,128)} %get-tuple-element.14), channel_id=1, source_target_pairs={{0,1},{1,2},{2,3},{4,5},{5,6},{6,7},{8,9},{9,10},{10,11},{12,13},{... | collective-permute-start | bytes 479240 | tf_op jit(solution)/shard_map/ppermute | solution.py:30
  69.5 76.1 %collective-permute-start.13 = (f32[2,312,64]{2,1,0:T(8,128)}, f32[2,312,64]{2,1,0:T(8,128)}, u32[]{:S(2)}, u32[]{:S(2)}) collective-permute-start(f32[2,312,64]{2,1,0:T(8,128)} %get-tuple-element.13), channel_id=1, source_target_pairs={{1,0},{2,1},{3,2},{5,4},{6,5},{7,6},{9,8},{10,9},{11,10},{13,12},{... | collective-permute-start | bytes 479240 | tf_op jit(solution)/shard_map/ppermute | solution.py:33
  85.2 26.9 %copy-start.2 = (f32[376,1152]{1,0:T(8,128)S(1)}, f32[376,1152]{1,0:T(8,128)}, u32[]{:S(2)}) copy-start(f32[376,1152]{1,0:T(8,128)} %get-tuple-element.3.l_ref) | copy-start | bytes 5197828
  85.2 26.9 %copy-start.3 = (f32[376,1152]{1,0:T(8,128)S(1)}, f32[376,1152]{1,0:T(8,128)}, u32[]{:S(2)}) copy-start(f32[376,1152]{1,0:T(8,128)} %get-tuple-element.4.c_ref) | copy-start | bytes 5197828
  116.1 34.3 %all-to-all-start = ((f32[4,46,128]{2,1,0:T(8,128)}), f32[4,46,128]{2,1,0:T(8,128)S(1)}, u32[]{:S(2)}, u32[]{:S(2)}) async-start(f32[4,46,128]{2,1,0:T(8,128)} %broadcast_in_dim.37), calls=%async_computation | async-start | bytes 196608 | tf_op jit(solution)/shard_map/all_to_all | solution.py:251
  120.6 29.9 %copy-start.27 = (pred[1152]{0:T(1024)(128)(4,1)S(1)}, pred[1152]{0:T(1024)(128)(4,1)}, u32[]{:S(2)}) copy-start(pred[1152]{0:T(1024)(128)(4,1)} %and.184) | copy-start | bytes 3460
  150.4 2.2 copy-start.19
  150.4 2.1 copy-start.23
  154.9 3.6 %copy-start = (f32[2,24,48,512]{3,2,1,0:T(8,128)}, f32[2,24,48,512]{3,2,1,0:T(8,128)S(1)}, u32[]{:S(2)}) copy-start(f32[2,24,48,512]{3,2,1,0:T(8,128)S(1)} %pad_maximum_fusion) | copy-start | bytes 14155780
  160.2 69.7 %copy-start.29 = (s32[8]{0:T(128)S(1)}, s32[8]{0:T(128)}, u32[]{:S(2)}) copy-start(s32[8]{0:T(128)} %iota_add_fusion.4) | copy-start | bytes 100
  232.1 6.2 %copy-start.5 = (f32[376,1152]{1,0:T(8,128)S(1)}, f32[376,1152]{1,0:T(8,128)}, u32[]{:S(2)}) copy-start(f32[376,1152]{1,0:T(8,128)} %shard_map.86) | copy-start | bytes 5197828
  232.1 8.7 %all-to-all-start.1 = ((f32[4,40,144]{2,1,0:T(8,128)}), f32[4,40,144]{2,1,0:T(8,128)S(1)}, u32[]{:S(2)}, u32[]{:S(2)}) async-start(f32[4,40,144]{2,1,0:T(8,128)} %pad_maximum_fusion.11), calls=%async_computation.1 | async-start | bytes 327680 | tf_op jit(solution)/shard_map/all_to_all | solution.py:280
  241.6 3.0 copy-start.8
  246.1 22.6 %copy-start.6 = (f32[312,1152]{1,0:T(8,128)S(1)}, f32[312,1152]{1,0:T(8,128)}, u32[]{:S(2)}) copy-start(f32[312,1152]{1,0:T(8,128)} %slice_divide_fusion.c_ref) | copy-start | bytes 4313092
  246.1 22.6 %copy-start.7 = (f32[312,1152]{1,0:T(8,128)S(1)}, f32[312,1152]{1,0:T(8,128)}, u32[]{:S(2)}) copy-start(f32[312,1152]{1,0:T(8,128)} %fusion.4.l_ref) | copy-start | bytes 4313092
  272.3 10.6 %all-to-all-start.2 = ((f32[4,38,128]{2,1,0:T(8,128)}), f32[4,38,128]{2,1,0:T(8,128)S(1)}, u32[]{:S(2)}, u32[]{:S(2)}) async-start(f32[4,38,128]{2,1,0:T(8,128)} %broadcast_in_dim.43), calls=%async_computation.2 | async-start | bytes 163840 | tf_op jit(solution)/shard_map/all_to_all | solution.py:251
  275.6 4.1 %copy-start.16 = (f32[1152,512]{1,0:T(8,128)S(1)}, f32[1152,512]{1,0:T(8,128)}, u32[]{:S(2)}) copy-start(f32[1152,512]{1,0:T(8,128)} %shard_map.87) | copy-start | bytes 7077892
  279.7 1.8 copy-start.9
  281.5 1.4 copy-start.28
where the time goes:
time: 329 us; the launch traced here: 326 us
  Pallas kernels  159 us (48%)
  local copies, waits for them, and re-layouts  55 us (17%)
  starting transfers between devices  50.3 us (15%)
  other arithmetic  32.7 us (10%)
  waiting for transfers between devices  26.3 us (8%)
    pallas_call x2, Pallas kernels, run_thermal(): pl.pallas_call(lambda *refs: thermal_kernel(*refs, stride=stride), out_sh...  109 us
    pallas_call x2, Pallas kernels, run_power(): pl.pallas_call(power_kernel, out_shape=jax.ShapeDtypeStruct((n, w), jnp.f...  49.5 us
    ppermute x7, waiting for transfers between devices, extended(): lax.ppermute(lax.slice_in_dim(block, 0, width, axis=dim), axis, backward)  25 us
    ppermute x7, starting transfers between devices, extended(): lax.ppermute(lax.slice_in_dim(block, block.shape[dim] - width, None, axis...  24.9 us
    ppermute x7, starting transfers between devices, extended(): lax.ppermute(lax.slice_in_dim(block, 0, width, axis=dim), axis, backward)  13.9 us
    concatenate x3, local copies, waits for them, and re-layouts, extended(): block = jnp.concatenate([low, block, high], axis=dim)  11.6 us
    concatenate x4, other arithmetic, extended(): block = jnp.concatenate([low, block, high], axis=dim)  9.58 us
    all_to_all x2, starting transfers between devices, gather_heat(): lax.all_to_all(copies, 'col', split_axis=0, concat_axis=0, tiled=True)  7.81 us
  transfers between devices with their start and end apart: 17, of which 2 were waited for; matrix products, arithmetic and copies ran while one was open for 18% of the time, Pallas kernels for 8%

commit v1 on v0

--- a/solution.py
+++ b/solution.py
@@ -1,3 +1,4 @@
+import functools
 import os
 
 import jax
@@ -59,13 +60,15 @@
 
 def row_above(x, above):
     sub = lax.broadcasted_iota(jnp.int32, x.shape, 0)
-    return jnp.where(sub == 0, pltpu.roll(above, 1, 0), pltpu.roll(x, 1, 0))
+    edge = jnp.broadcast_to(above[x.shape[0] - 1:, :], x.shape)
+    return jnp.where(sub == 0, edge, pltpu.roll(x, 1, 0))
 
 
 def row_below(x, below):
     n = x.shape[0]
     sub = lax.broadcasted_iota(jnp.int32, x.shape, 0)
-    return jnp.where(sub == n - 1, pltpu.roll(below, n - 1, 0), pltpu.roll(x, n - 1, 0))
+    edge = jnp.broadcast_to(below[:1, :], x.shape)
+    return jnp.where(sub == n - 1, edge, pltpu.roll(x, n - 1, 0))
 
 
 def rows_of(k):
@@ -76,7 +79,7 @@
     return ref[rows_of(jnp.clip(k, 0, count - 1)), :]
 
 
-def power_kernel(d_ref, c_ref, l_ref, v_ref, rok_ref, cok_ref, o_ref, wn_ref, ws_ref, ww_ref, we_ref, den_ref, buf_ref):
+def power_kernel(d_ref, c_ref, l_ref, v_ref, rok_ref, cok_ref, o_ref, wn_ref, ws_ref, ww_ref, we_ref, inv_ref, buf_ref):
     n, w = c_ref.shape
     count = n // 8
 
@@ -91,11 +94,11 @@
         ws_ref[sl, :] = b
         ww_ref[sl, :] = e
         we_ref[sl, :] = f
-        den_ref[sl, :] = a + b + e + f + v_ref[sl, :]
+        ok = (rok_ref[sl, :] > 0.5) & (cok_ref[...] > 0.5)
+        inv_ref[sl, :] = jnp.where(ok, 1.0 / (a + b + e + f + v_ref[sl, :]), 0.0)
         return carry
 
     lax.fori_loop(0, count, weights, 0)
-    col_ok = cok_ref[...] > 0.5
 
     def sweep(src, dst):
         def body(k, carry):
@@ -108,8 +111,8 @@
                 + ww_ref[sl, :] * pltpu.roll(x, 1, 1)
                 + we_ref[sl, :] * pltpu.roll(x, w - 1, 1)
             )
-            ok = (rok_ref[sl, :] > 0.5) & col_ok
-            dst[sl, :] = jnp.where(ok, summed / den_ref[sl, :], 0.0)
+            inv = inv_ref[sl, :]
+            dst[sl, :] = jnp.where(inv != 0.0, summed * inv, 0.0)
             return carry
 
         lax.fori_loop(0, count, body, 0)
@@ -131,12 +134,16 @@
     )(drop, cond, load, via, row_ok, col_ok)
 
 
-def thermal_kernel(t_ref, s_ref, lk_ref, vk_ref, rok_ref, o_ref, wb_ref, wa_ref, den_ref, buf_ref, *, stride):
+def thermal_kernel(t_ref, s_ref, lk_ref, vk_ref, rok_ref, o_ref, *scratch, stride, stored):
     n, w = lk_ref.shape
     count = n // 8
     lane = lax.broadcasted_iota(jnp.int32, (8, w), 1)
     first = lane == 0
     last = lane == w - 1
+    if stored:
+        wn_ref, ws_ref, ww_ref, we_ref, wb_ref, wa_ref, inv_ref, buf_ref = scratch
+    else:
+        wb_ref, wa_ref, inv_ref, buf_ref = scratch
 
     def lateral(x, k, ref):
         up = row_above(x, chunk(ref, k - 1, count))
@@ -145,16 +152,26 @@
         rt = jnp.where(last, 0.0, pltpu.roll(x, w - 1, 1))
         return up, dn, lf, rt
 
-    def weights(k, carry):
+    def lateral_weights(k):
         sl = rows_of(k)
         x = lk_ref[sl, :]
         up, dn, lf, rt = lateral(x, k, lk_ref)
+        return (x + up) * 0.5, (x + dn) * 0.5, (x + lf) * 0.5, (x + rt) * 0.5
+
+    def weights(k, carry):
+        sl = rows_of(k)
+        a, b, e, f = lateral_weights(k)
+        if stored:
+            wn_ref[sl, :] = a
+            ws_ref[sl, :] = b
+            ww_ref[sl, :] = e
+            we_ref[sl, :] = f
         v = vk_ref[sl, :]
-        b = (v + chunk(vk_ref, k - stride, count)) * 0.5
-        a = (v + chunk(vk_ref, k + stride, count)) * 0.5
-        wb_ref[sl, :] = b
-        wa_ref[sl, :] = a
-        den_ref[sl, :] = (x + up) * 0.5 + (x + dn) * 0.5 + (x + lf) * 0.5 + (x + rt) * 0.5 + b + a
+        lo = (v + chunk(vk_ref, k - stride, count)) * 0.5
+        hi = (v + chunk(vk_ref, k + stride, count)) * 0.5
+        wb_ref[sl, :] = lo
+        wa_ref[sl, :] = hi
+        inv_ref[sl, :] = jnp.where(rok_ref[sl, :] > 0.5, 1.0 / (a + b + e + f + lo + hi), 0.0)
         return carry
 
     lax.fori_loop(0, count, weights, 0)
@@ -162,20 +179,23 @@
     def sweep(src, dst):
         def body(k, carry):
             sl = rows_of(k)
-            lk = lk_ref[sl, :]
-            kup, kdn, klf, krt = lateral(lk, k, lk_ref)
+            if stored:
+                a, b, e, f = wn_ref[sl, :], ws_ref[sl, :], ww_ref[sl, :], we_ref[sl, :]
+            else:
+                a, b, e, f = lateral_weights(k)
             x = src[sl, :]
             up, dn, lf, rt = lateral(x, k, src)
             summed = (
                 s_ref[sl, :]
-                + (lk + kup) * 0.5 * up
-                + (lk + kdn) * 0.5 * dn
-                + (lk + klf) * 0.5 * lf
-                + (lk + krt) * 0.5 * rt
+                + a * up
+                + b * dn
+                + e * lf
+                + f * rt
                 + wb_ref[sl, :] * chunk(src, k - stride, count)
                 + wa_ref[sl, :] * chunk(src, k + stride, count)
             )
-            dst[sl, :] = jnp.where(rok_ref[sl, :] > 0.5, summed / den_ref[sl, :], 0.0)
+            inv = inv_ref[sl, :]
+            dst[sl, :] = jnp.where(inv != 0.0, summed * inv, 0.0)
             return carry
 
         lax.fori_loop(0, count, body, 0)
@@ -188,10 +208,12 @@
 
 def run_thermal(temp, source, lat, vert, row_ok, stride):
     n, w = lat.shape
+    stored = 13 * n * w * 4 <= 40 * 1024 * 1024
+    kernel = functools.partial(thermal_kernel, stride=stride, stored=stored)
     return pl.pallas_call(
-        lambda *refs: thermal_kernel(*refs, stride=stride),
+        kernel,
         out_shape=jax.ShapeDtypeStruct((n, w), jnp.float32),
-        scratch_shapes=[pltpu.VMEM((n, w), jnp.float32) for _ in range(4)],
+        scratch_shapes=[pltpu.VMEM((n, w), jnp.float32) for _ in range(8 if stored else 4)],
         compiler_params=pltpu.CompilerParams(vmem_limit_bytes=60 * 1024 * 1024),
         interpret=INTERPRET,
     )(temp, source, lat, vert, row_ok)

time: 329 us -> 322 us (0.979)
  Pallas kernels: 159 us -> 151 us
    pallas_call x2, Pallas kernels: 109 us -> 102 us  [run_thermal(): pl.pallas_call(kernel, out_shape=jax.ShapeDtypeStruct((n, w), jnp.float32...]
where the time goes in v1:
time: 322 us; the launch traced here: 318 us
  Pallas kernels  151 us (47%)
  local copies, waits for them, and re-layouts  55 us (17%)
  starting transfers between devices  50.3 us (16%)
  other arithmetic  32.7 us (10%)
  waiting for transfers between devices  26.8 us (8%)
    pallas_call x2, Pallas kernels, run_thermal(): pl.pallas_call(kernel, out_shape=jax.ShapeDtypeStruct((n, w), jnp.float32...  102 us
    pallas_call x2, Pallas kernels, run_power(): pl.pallas_call(power_kernel, out_shape=jax.ShapeDtypeStruct((n, w), jnp.f...  48.6 us
    ppermute x7, waiting for transfers between devices, extended(): lax.ppermute(lax.slice_in_dim(block, 0, width, axis=dim), axis, backward)  25.5 us
    ppermute x7, starting transfers between devices, extended(): lax.ppermute(lax.slice_in_dim(block, block.shape[dim] - width, None, axis...  24.9 us
    ppermute x7, starting transfers between devices, extended(): lax.ppermute(lax.slice_in_dim(block, 0, width, axis=dim), axis, backward)  13.9 us
    concatenate x3, local copies, waits for them, and re-layouts, extended(): block = jnp.concatenate([low, block, high], axis=dim)  11.6 us
    concatenate x4, other arithmetic, extended(): block = jnp.concatenate([low, block, high], axis=dim)  9.58 us
    all_to_all x2, starting transfers between devices, gather_heat(): lax.all_to_all(copies, 'col', split_axis=0, concat_axis=0, tiled=True)  7.81 us
  transfers between devices with their start and end apart: 17, of which 2 were waited for; matrix products, arithmetic and copies ran while one was open for 18% of the time, Pallas kernels for 8%

profile of v1, /device:TPU:8, one launch (start us, length us, event | category | flops | bytes accessed | tf_op | source)
XLA Modules:
  0.0 318.3 jit_solution(4285382990363584278)
XLA Ops:
  0.7 1.5 multiply_bitcast_fusion
  2.7 0.8 copy-done.14
  3.5 1.0 copy-done.20
  4.5 1.3 pad_maximum_fusion.6
  5.8 2.1 collective-permute-start.1
  7.9 2.4 collective-permute-start
  10.9 3.1 collective-permute-start.4
  14.1 2.5 collective-permute-start.11
  16.5 1.9 collective-permute-start.10
  19.1 0.7 fusion.19.rok_ref
  19.8 0.7 fusion.23.rok_ref
  20.5 0.8 pad_maximum_fusion.10
  22.5 1.1 reshape.293.rok_ref
  24.1 0.9 reshape.294.rok_ref
  26.2 3.6 %collective-permute-start.5 = (s32[8,512]{1,0:T(8,128)}, s32[8,512]{1,0:T(8,128)S(1)}, u32[]{:S(2)}, u32[]{:S(2)}) collective-permute-start(s32[8,512]{1,0:T(8,128)} %get-tuple-element.23), channel_id=1, source_target_pairs={{4,0},{8,4},{12,8},{16,12},{20,16},{24,20},{28,24},{5,1},{9,5},{13... | collective-permute-start | bytes 49160 | tf_op jit(solution)/shard_map/ppermute | solution.py:34
  29.9 1.9 collective-permute-start.7
  31.8 0.7 copy-done.25
  32.5 2.7 collective-permute-start.6
  35.2 2.0 pad_maximum_fusion.2
  37.2 2.8 pad_maximum_fusion.1
  40.0 2.1 copy-done.1
  42.1 1.2 fusion.44
  43.3 2.0 copy.33
  45.3 4.1 %collective-permute-start.2 = (f32[3,376,64]{1,2,0:T(8,128)}, f32[3,376,64]{1,2,0:T(8,128)}, u32[]{:S(2)}, u32[]{:S(2)}) collective-permute-start(f32[3,376,64]{1,2,0:T(8,128)} %copy.33), channel_id=1, source_target_pairs={{0,1},{1,2},{2,3},{4,5},{5,6},{6,7},{8,9},{9,10},{10,11},{12,13},{... | collective-permute-start | bytes 866312 | tf_op jit(solution)/shard_map/ppermute | solution.py:31
  49.5 2.0 copy.34
  51.4 1.3 collective-permute-start.3
  52.8 2.5 pad_maximum_fusion.3
  55.3 1.3 collective-permute-start.9
  56.6 6.3 %collective-permute-start.8 = (f32[2,8,48,512]{3,2,1,0:T(8,128)}, f32[2,8,48,512]{3,2,1,0:T(8,128)}, u32[]{:S(2)}, u32[]{:S(2)}) collective-permute-start(f32[2,8,48,512]{3,2,1,0:T(8,128)} %pad_maximum_fusion.3), channel_id=1, source_target_pairs={{0,1},{1,2},{2,3},{4,5},{5,6},{6,7},{8,9},{9,10},{10,11},{12,13},{... | collective-permute-start | bytes 4718600 | tf_op jit(solution)/shard_map/ppermute | solution.py:31
  62.9 0.9 fusion.45
  63.9 4.4 %collective-permute-start.12 = (f32[2,312,64]{2,1,0:T(8,128)}, f32[2,312,64]{2,1,0:T(8,128)}, u32[]{:S(2)}, u32[]{:S(2)}) collective-permute-start(f32[2,312,64]{2,1,0:T(8,128)} %get-tuple-element.14), channel_id=1, source_target_pairs={{0,1},{1,2},{2,3},{4,5},{5,6},{6,7},{8,9},{9,10},{10,11},{12,13},{... | collective-permute-start | bytes 479240 | tf_op jit(solution)/shard_map/ppermute | solution.py:31
  68.3 1.2 copy.35
  69.5 1.3 collective-permute-start.13
  70.8 1.2 copy.36
  72.0 6.9 %concatenate.22 = f32[3,376,1152]{2,1,0:T(8,128)} concatenate(f32[3,376,64]{2,1,0:T(8,128)S(1)} %copy.35, f32[3,376,1024]{2,1,0:T(8,128)} %copy-done.1, f32[3,376,64]{2,1,0:T(8,128)S(1)} %copy.36), dimensions={2} | concatenate | bytes 10395648 | tf_op jit(solution)/shard_map/concatenate | solution.py:35
  78.9 4.9 %slice_bitcast_fusion = (f32[376,1152]{1,0:T(8,128)}, f32[376,1152]{1,0:T(8,128)}, f32[376,1152]{1,0:T(8,128)}) fusion(f32[3,376,1152]{2,1,0:T(8,128)} %concatenate.22), kind=kLoop, calls=%fused_computation.8 | loop fusion | bytes 10395648 | tf_op jit(solution)/shard_map/squeeze | solution.py:264
  83.8 1.3 broadcast_in_dim.36.d_ref
  85.2 26.4 %shard_map.86 = f32[376,1152]{1,0:T(8,128)} custom-call(f32[376,1152]{1,0:T(8,128)} %broadcast_in_dim.36.d_ref, f32[376,1152]{1,0:T(8,128)} %get-tuple-element.4.c_ref, f32[376,1152]{1,0:T(8,128)} %get-tuple-element.3.l_ref, f32[376,1152]{1,0:T(8,128)} %get-tuple-element.2.v_ref, f32[376,1]{1,0:T(8,128)} %fusion.19.rok_ref, f32[1,1152]{1,0:T(1,128)} %and_convert_fusion.cok_ref), custom_call_target="tpu_custom_call" | custom-call | tf_op jit(solution)/shard_map/pallas_call | solution.py:128
  111.6 2.9 fusion.3
  115.5 4.5 %all-to-all-start = ((f32[4,46,128]{2,1,0:T(8,128)}), f32[4,46,128]{2,1,0:T(8,128)S(1)}, u32[]{:S(2)}, u32[]{:S(2)}) async-start(f32[4,46,128]{2,1,0:T(8,128)} %broadcast_in_dim.37), calls=%async_computation | async-start | bytes 196608 | tf_op jit(solution)/shard_map/all_to_all | solution.py:273
  120.1 25.5 %collective-permute-done.13 = f32[2,312,64]{2,1,0:T(8,128)} collective-permute-done((f32[2,312,64]{2,1,0:T(8,128)}, f32[2,312,64]{2,1,0:T(8,128)}, u32[]{:S(2)}, u32[]{:S(2)}) %collective-permute-start.13) | collective-permute-done | bytes 159776 | tf_op jit(solution)/shard_map/ppermute | solution.py:34
  145.6 4.7 %concatenate.27 = f32[2,312,1152]{2,1,0:T(8,128)} concatenate(f32[2,312,64]{2,1,0:T(8,128)} %collective-permute-done.12, f32[2,312,1024]{2,1,0:T(8,128)} %copy-done.4, f32[2,312,64]{2,1,0:T(8,128)} %collective-permute-done.13), dimensions={2} | concatenate | bytes 5750784 | tf_op jit(solution)/shard_map/concatenate | solution.py:35
  150.5 2.1 bitcast_select_fusion.s_ref
  152.6 2.3 pad_maximum_fusion
  154.9 3.5 %fusion.43 = (f32[1,24,48,512]{3,2,1,0:T(8,128)}, f32[1,24,48,512]{3,2,1,0:T(8,128)}) fusion(f32[2,24,48,512]{3,2,1,0:T(8,128)S(1)} %pad_maximum_fusion), kind=kLoop, calls=%fused_computation.108 | loop fusion | bytes 9437184 | tf_op jit(solution)/shard_map/slice | solution.py:288
  158.5 1.7 reshape.281.t_ref
  160.2 65.2 %shard_map.87 = f32[1152,512]{1,0:T(8,128)} custom-call(f32[1152,512]{1,0:T(8,128)} %reshape.281.t_ref, f32[1152,512]{1,0:T(8,128)} %bitcast_select_fusion.s_ref, f32[1152,512]{1,0:T(8,128)} %bitcast.91, f32[1152,512]{1,0:T(8,128)} %bitcast.90, f32[1152,1]{1,0:T(8,128)} %reshape.293.rok_ref), custom_call_target="tpu_custom_call" | custom-call | tf_op jit(solution)/shard_map/pallas_call | solution.py:213
  225.4 1.3 fusion.11
  226.8 0.7 pad_maximum_fusion.11
  227.5 3.7 %all-to-all-start.1 = ((f32[4,40,144]{2,1,0:T(8,128)}), f32[4,40,144]{2,1,0:T(8,128)S(1)}, u32[]{:S(2)}, u32[]{:S(2)}) async-start(f32[4,40,144]{2,1,0:T(8,128)} %pad_maximum_fusion.11), calls=%async_computation.1 | async-start | bytes 327680 | tf_op jit(solution)/shard_map/all_to_all | solution.py:302
  231.2 2.5 slice_bitcast_fusion.3.v_ref
  233.7 1.3 slice.190.d_ref
  235.0 1.3 all-to-all-done.1
  237.1 2.9 slice_divide_fusion.c_ref
  240.1 1.5 fusion.4.l_ref
  241.5 22.2 %shard_map.88 = f32[312,1152]{1,0:T(8,128)} custom-call(f32[312,1152]{1,0:T(8,128)} %slice.190.d_ref, f32[312,1152]{1,0:T(8,128)} %slice_divide_fusion.c_ref, f32[312,1152]{1,0:T(8,128)} %fusion.4.l_ref, f32[312,1152]{1,0:T(8,128)} %slice_bitcast_fusion.3.v_ref, f32[312,1]{1,0:T(8,128)} %fusion.23.rok_ref, f32[1,1152]{1,0:T(1,128)} %and_convert_fusion.cok_ref), custom_call_target="tpu_custom_call" | custom-call | tf_op jit(solution)/shard_map/pallas_call | solution.py:128
  263.7 2.5 fusion.8
  267.3 3.3 %all-to-all-start.2 = ((f32[4,38,128]{2,1,0:T(8,128)}), f32[4,38,128]{2,1,0:T(8,128)S(1)}, u32[]{:S(2)}, u32[]{:S(2)}) async-start(f32[4,38,128]{2,1,0:T(8,128)} %broadcast_in_dim.43), calls=%async_computation.2 | async-start | bytes 163840 | tf_op jit(solution)/shard_map/all_to_all | solution.py:273
  270.6 4.1 %fusion.42 = (f32[1,16,40,512]{3,2,1,0:T(8,128)}, f32[1,16,40,512]{3,2,1,0:T(8,128)}) fusion(f32[2,24,48,512]{3,2,1,0:T(8,128)} %copy-done), kind=kLoop, calls=%fused_computation.107 | loop fusion | bytes 5242880 | tf_op jit(solution)/shard_map/slice | solution.py:288
  274.7 1.2 slice.209
  276.6 1.3 slice.208
  278.0 1.4 bitcast_select_fusion.1.s_ref
  279.4 37.0 %shard_map.89 = f32[640,512]{1,0:T(8,128)} custom-call(f32[640,512]{1,0:T(8,128)} %bitcast.96, f32[640,512]{1,0:T(8,128)} %bitcast_select_fusion.1.s_ref, f32[640,512]{1,0:T(8,128)} %bitcast.95, f32[640,512]{1,0:T(8,128)} %bitcast.94, f32[640,1]{1,0:T(8,128)} %reshape.294.rok_ref), custom_call_target="tpu_custom_call" | custom-call | tf_op jit(solution)/shard_map/pallas_call | solution.py:213
  316.4 1.9 slice.215
  (122 shorter events, 8.7 us)
Async XLA Ops:
  0.6 1.5 copy-start.10
  0.6 1.8 copy-start.11
  2.5 1.0 copy-start.14
  2.5 2.0 copy-start.20
  2.7 3.1 copy-start.12
  4.5 5.8 %copy-start.26 = (s32[32,512]{1,0:T(8,128)S(1)}, s32[32,512]{1,0:T(8,128)}, u32[]{:S(2)}) copy-start(s32[32,512]{1,0:T(8,128)} %param.11) | copy-start | bytes 196612
  5.8 14.7 %copy-start.17 = (f32[8,32,512]{2,1,0:T(8,128)S(1)}, f32[8,32,512]{2,1,0:T(8,128)}, u32[]{:S(2)}) copy-start(f32[8,32,512]{2,1,0:T(8,128)} %param.13) | copy-start | bytes 1572868
  5.8 14.7 %copy-start.18 = (f32[8,32,512]{2,1,0:T(8,128)S(1)}, f32[8,32,512]{2,1,0:T(8,128)}, u32[]{:S(2)}) copy-start(f32[8,32,512]{2,1,0:T(8,128)} %param.12) | copy-start | bytes 1572868
  5.8 31.3 %collective-permute-start.1 = (f32[3,60,1024]{2,1,0:T(8,128)}, f32[3,60,1024]{2,1,0:T(8,128)}, u32[]{:S(2)}, u32[]{:S(2)}) collective-permute-start(f32[3,60,1024]{2,1,0:T(8,128)} %get-tuple-element.12), channel_id=1, source_target_pairs={{4,0},{8,4},{12,8},{16,12},{20,16},{24,20},{28,24},{5,1},{9,5},{13... | collective-permute-start | bytes 2211848 | tf_op jit(solution)/shard_map/ppermute | solution.py:34
  7.9 29.3 %collective-permute-start = (f32[3,60,1024]{2,1,0:T(8,128)}, f32[3,60,1024]{2,1,0:T(8,128)}, u32[]{:S(2)}, u32[]{:S(2)}) collective-permute-start(f32[3,60,1024]{2,1,0:T(8,128)} %get-tuple-element.11), channel_id=1, source_target_pairs={{0,4},{4,8},{8,12},{12,16},{16,20},{20,24},{24,28},{1,5},{5,9},{9,... | collective-permute-start | bytes 2211848 | tf_op jit(solution)/shard_map/ppermute | solution.py:31
  10.9 15.3 %collective-permute-start.4 = (s32[8,512]{1,0:T(8,128)S(1)}, s32[8,512]{1,0:T(8,128)S(1)}, u32[]{:S(2)}, u32[]{:S(2)}) collective-permute-start(s32[8,512]{1,0:T(8,128)S(1)} %get-tuple-element.24), channel_id=1, source_target_pairs={{0,4},{4,8},{8,12},{12,16},{16,20},{20,24},{24,28},{1,5},{5,9},{9,... | collective-permute-start | bytes 49160 | tf_op jit(solution)/shard_map/ppermute | solution.py:31
  14.1 15.8 %collective-permute-start.11 = (f32[2,28,1024]{2,1,0:T(8,128)S(1)}, f32[2,28,1024]{2,1,0:T(8,128)S(1)}, u32[]{:S(2)}, u32[]{:S(2)}) collective-permute-start(f32[2,28,1024]{2,1,0:T(8,128)S(1)} %get-tuple-element.16), channel_id=1, source_target_pairs={{4,0},{8,4},{12,8},{16,12},{20,16},{24,20},{28,24},{5,1},{9,5},{13... | collective-permute-start | bytes 688136 | tf_op jit(solution)/shard_map/ppermute | solution.py:34
  16.5 15.3 %collective-permute-start.10 = (f32[2,28,1024]{2,1,0:T(8,128)S(1)}, f32[2,28,1024]{2,1,0:T(8,128)S(1)}, u32[]{:S(2)}, u32[]{:S(2)}) collective-permute-start(f32[2,28,1024]{2,1,0:T(8,128)S(1)} %get-tuple-element.15), channel_id=1, source_target_pairs={{0,4},{4,8},{8,12},{12,16},{16,20},{20,24},{24,28},{1,5},{5,9},{9,... | collective-permute-start | bytes 688136 | tf_op jit(solution)/shard_map/ppermute | solution.py:31
  26.2 93.9 %collective-permute-start.5 = (s32[8,512]{1,0:T(8,128)}, s32[8,512]{1,0:T(8,128)S(1)}, u32[]{:S(2)}, u32[]{:S(2)}) collective-permute-start(s32[8,512]{1,0:T(8,128)} %get-tuple-element.23), channel_id=1, source_target_pairs={{4,0},{8,4},{12,8},{16,12},{20,16},{24,20},{28,24},{5,1},{9,5},{13... | collective-permute-start | bytes 49160 | tf_op jit(solution)/shard_map/ppermute | solution.py:34
  29.8 2.0 copy-start.24
  29.9 22.9 %collective-permute-start.7 = (f32[2,8,8,512]{3,2,1,0:T(8,128)}, f32[2,8,8,512]{3,2,1,0:T(8,128)S(1)}, u32[]{:S(2)}, u32[]{:S(2)}) collective-permute-start(f32[2,8,8,512]{3,2,1,0:T(8,128)} %get-tuple-element.18), channel_id=1, source_target_pairs={{4,0},{8,4},{12,8},{16,12},{20,16},{24,20},{28,24},{5,1},{9,5},{13... | collective-permute-start | bytes 786440 | tf_op jit(solution)/shard_map/ppermute | solution.py:34
  31.8 0.7 copy-start.25
  32.5 4.7 %copy-start.13 = (f32[1,256,1024]{2,1,0:T(8,128)S(1)}, f32[1,256,1024]{2,1,0:T(8,128)}, u32[]{:S(2)}) copy-start(f32[1,256,1024]{2,1,0:T(8,128)} %copy-done.12) | copy-start | bytes 3145732
  32.5 4.7 %copy-start.15 = (f32[1,256,1024]{2,1,0:T(8,128)S(1)}, f32[1,256,1024]{2,1,0:T(8,128)}, u32[]{:S(2)}) copy-start(f32[1,256,1024]{2,1,0:T(8,128)} %copy-done.14) | copy-start | bytes 3145732
  32.5 4.7 %copy-start.21 = (f32[256,1024]{1,0:T(8,128)S(1)}, f32[256,1024]{1,0:T(8,128)}, u32[]{:S(2)}) copy-start(f32[256,1024]{1,0:T(8,128)} %param.9) | copy-start | bytes 3145732
  32.5 20.3 %collective-permute-start.6 = (f32[2,8,8,512]{3,2,1,0:T(8,128)}, f32[2,8,8,512]{3,2,1,0:T(8,128)}, u32[]{:S(2)}, u32[]{:S(2)}) collective-permute-start(f32[2,8,8,512]{3,2,1,0:T(8,128)} %get-tuple-element.17), channel_id=1, source_target_pairs={{0,4},{4,8},{8,12},{12,16},{16,20},{20,24},{24,28},{1,5},{5,9},{9,... | collective-permute-start | bytes 786440 | tf_op jit(solution)/shard_map/ppermute | solution.py:31
  37.1 25.8 %copy-start.4 = (f32[2,312,1024]{2,1,0:T(8,128)}, f32[2,312,1024]{2,1,0:T(8,128)S(1)}, u32[]{:S(2)}) copy-start(f32[2,312,1024]{2,1,0:T(8,128)S(1)} %pad_maximum_fusion.2) | copy-start | bytes 7667716
  40.0 2.2 copy-start.1
  45.3 18.5 %collective-permute-start.2 = (f32[3,376,64]{1,2,0:T(8,128)}, f32[3,376,64]{1,2,0:T(8,128)}, u32[]{:S(2)}, u32[]{:S(2)}) collective-permute-start(f32[3,376,64]{1,2,0:T(8,128)} %copy.33), channel_id=1, source_target_pairs={{0,1},{1,2},{2,3},{4,5},{5,6},{6,7},{8,9},{9,10},{10,11},{12,13},{... | collective-permute-start | bytes 866312 | tf_op jit(solution)/shard_map/ppermute | solution.py:31
  51.4 18.0 %collective-permute-start.3 = (f32[3,376,64]{1,2,0:T(8,128)}, f32[3,376,64]{1,2,0:T(8,128)}, u32[]{:S(2)}, u32[]{:S(2)}) collective-permute-start(f32[3,376,64]{1,2,0:T(8,128)} %copy.34), channel_id=1, source_target_pairs={{1,0},{2,1},{3,2},{5,4},{6,5},{7,6},{9,8},{10,9},{11,10},{13,12},{... | collective-permute-start | bytes 866312 | tf_op jit(solution)/shard_map/ppermute | solution.py:34
  52.7 2.5 copy-start.22
  55.3 97.2 %collective-permute-start.9 = (f32[2,8,48,512]{3,2,1,0:T(8,128)}, f32[2,8,48,512]{3,2,1,0:T(8,128)}, u32[]{:S(2)}, u32[]{:S(2)}) collective-permute-start(f32[2,8,48,512]{3,2,1,0:T(8,128)} %pad_maximum_fusion.3), channel_id=1, source_target_pairs={{1,0},{2,1},{3,2},{5,4},{6,5},{7,6},{9,8},{10,9},{11,10},{13,12},{... | collective-permute-start | bytes 4718600 | tf_op jit(solution)/shard_map/ppermute | solution.py:34
  56.6 96.0 %collective-permute-start.8 = (f32[2,8,48,512]{3,2,1,0:T(8,128)}, f32[2,8,48,512]{3,2,1,0:T(8,128)}, u32[]{:S(2)}, u32[]{:S(2)}) collective-permute-start(f32[2,8,48,512]{3,2,1,0:T(8,128)} %pad_maximum_fusion.3), channel_id=1, source_target_pairs={{0,1},{1,2},{2,3},{4,5},{5,6},{6,7},{8,9},{9,10},{10,11},{12,13},{... | collective-permute-start | bytes 4718600 | tf_op jit(solution)/shard_map/ppermute | solution.py:31
  63.9 56.3 %collective-permute-start.12 = (f32[2,312,64]{2,1,0:T(8,128)}, f32[2,312,64]{2,1,0:T(8,128)}, u32[]{:S(2)}, u32[]{:S(2)}) collective-permute-start(f32[2,312,64]{2,1,0:T(8,128)} %get-tuple-element.14), channel_id=1, source_target_pairs={{0,1},{1,2},{2,3},{4,5},{5,6},{6,7},{8,9},{9,10},{10,11},{12,13},{... | collective-permute-start | bytes 479240 | tf_op jit(solution)/shard_map/ppermute | solution.py:31
  69.5 76.1 %collective-permute-start.13 = (f32[2,312,64]{2,1,0:T(8,128)}, f32[2,312,64]{2,1,0:T(8,128)}, u32[]{:S(2)}, u32[]{:S(2)}) collective-permute-start(f32[2,312,64]{2,1,0:T(8,128)} %get-tuple-element.13), channel_id=1, source_target_pairs={{1,0},{2,1},{3,2},{5,4},{6,5},{7,6},{9,8},{10,9},{11,10},{13,12},{... | collective-permute-start | bytes 479240 | tf_op jit(solution)/shard_map/ppermute | solution.py:34
  85.2 26.4 %copy-start.2 = (f32[376,1152]{1,0:T(8,128)S(1)}, f32[376,1152]{1,0:T(8,128)}, u32[]{:S(2)}) copy-start(f32[376,1152]{1,0:T(8,128)} %get-tuple-element.3.l_ref) | copy-start | bytes 5197828
  85.2 26.4 %copy-start.3 = (f32[376,1152]{1,0:T(8,128)S(1)}, f32[376,1152]{1,0:T(8,128)}, u32[]{:S(2)}) copy-start(f32[376,1152]{1,0:T(8,128)} %get-tuple-element.4.c_ref) | copy-start | bytes 5197828
  115.5 34.8 %all-to-all-start = ((f32[4,46,128]{2,1,0:T(8,128)}), f32[4,46,128]{2,1,0:T(8,128)S(1)}, u32[]{:S(2)}, u32[]{:S(2)}) async-start(f32[4,46,128]{2,1,0:T(8,128)} %broadcast_in_dim.37), calls=%async_computation | async-start | bytes 196608 | tf_op jit(solution)/shard_map/all_to_all | solution.py:273
  120.1 30.4 %copy-start.27 = (pred[1152]{0:T(1024)(128)(4,1)S(1)}, pred[1152]{0:T(1024)(128)(4,1)}, u32[]{:S(2)}) copy-start(pred[1152]{0:T(1024)(128)(4,1)} %and.184) | copy-start | bytes 3460
  150.4 2.2 copy-start.19
  150.4 2.1 copy-start.23
  154.9 3.6 %copy-start = (f32[2,24,48,512]{3,2,1,0:T(8,128)}, f32[2,24,48,512]{3,2,1,0:T(8,128)S(1)}, u32[]{:S(2)}) copy-start(f32[2,24,48,512]{3,2,1,0:T(8,128)S(1)} %pad_maximum_fusion) | copy-start | bytes 14155780
  160.2 65.2 %copy-start.29 = (s32[8]{0:T(128)S(1)}, s32[8]{0:T(128)}, u32[]{:S(2)}) copy-start(s32[8]{0:T(128)} %iota_add_fusion.4) | copy-start | bytes 100
  227.5 6.2 %copy-start.5 = (f32[376,1152]{1,0:T(8,128)S(1)}, f32[376,1152]{1,0:T(8,128)}, u32[]{:S(2)}) copy-start(f32[376,1152]{1,0:T(8,128)} %shard_map.86) | copy-start | bytes 5197828
  227.5 8.7 %all-to-all-start.1 = ((f32[4,40,144]{2,1,0:T(8,128)}), f32[4,40,144]{2,1,0:T(8,128)S(1)}, u32[]{:S(2)}, u32[]{:S(2)}) async-start(f32[4,40,144]{2,1,0:T(8,128)} %pad_maximum_fusion.11), calls=%async_computation.1 | async-start | bytes 327680 | tf_op jit(solution)/shard_map/all_to_all | solution.py:302
  237.1 3.0 copy-start.8
  241.5 22.2 %copy-start.6 = (f32[312,1152]{1,0:T(8,128)S(1)}, f32[312,1152]{1,0:T(8,128)}, u32[]{:S(2)}) copy-start(f32[312,1152]{1,0:T(8,128)} %slice_divide_fusion.c_ref) | copy-start | bytes 4313092
  241.5 22.2 %copy-start.7 = (f32[312,1152]{1,0:T(8,128)S(1)}, f32[312,1152]{1,0:T(8,128)}, u32[]{:S(2)}) copy-start(f32[312,1152]{1,0:T(8,128)} %fusion.4.l_ref) | copy-start | bytes 4313092
  267.3 10.6 %all-to-all-start.2 = ((f32[4,38,128]{2,1,0:T(8,128)}), f32[4,38,128]{2,1,0:T(8,128)S(1)}, u32[]{:S(2)}, u32[]{:S(2)}) async-start(f32[4,38,128]{2,1,0:T(8,128)} %broadcast_in_dim.43), calls=%async_computation.2 | async-start | bytes 163840 | tf_op jit(solution)/shard_map/all_to_all | solution.py:273
  270.6 4.1 %copy-start.16 = (f32[1152,512]{1,0:T(8,128)S(1)}, f32[1152,512]{1,0:T(8,128)}, u32[]{:S(2)}) copy-start(f32[1152,512]{1,0:T(8,128)} %shard_map.87) | copy-start | bytes 7077892
  274.7 1.8 copy-start.9
  276.6 1.4 copy-start.28

commit v2 on v1

--- a/solution.py
+++ b/solution.py
@@ -9,6 +9,7 @@
 from jax.sharding import PartitionSpec as P
 
 INTERPRET = os.environ.get("SOL_INTERPRET") == "1"
+UNROLL = 4
 
 COARSE = 8
 SWEEPS = 4
@@ -98,7 +99,7 @@
         inv_ref[sl, :] = jnp.where(ok, 1.0 / (a + b + e + f + v_ref[sl, :]), 0.0)
         return carry
 
-    lax.fori_loop(0, count, weights, 0)
+    lax.fori_loop(0, count, weights, 0, unroll=UNROLL)
 
     def sweep(src, dst):
         def body(k, carry):
@@ -115,7 +116,7 @@
             dst[sl, :] = jnp.where(inv != 0.0, summed * inv, 0.0)
             return carry
 
-        lax.fori_loop(0, count, body, 0)
+        lax.fori_loop(0, count, body, 0, unroll=UNROLL)
 
     sweep(d_ref, buf_ref)
     sweep(buf_ref, o_ref)
@@ -174,7 +175,7 @@
         inv_ref[sl, :] = jnp.where(rok_ref[sl, :] > 0.5, 1.0 / (a + b + e + f + lo + hi), 0.0)
         return carry
 
-    lax.fori_loop(0, count, weights, 0)
+    lax.fori_loop(0, count, weights, 0, unroll=UNROLL)
 
     def sweep(src, dst):
         def body(k, carry):
@@ -198,7 +199,7 @@
             dst[sl, :] = jnp.where(inv != 0.0, summed * inv, 0.0)
             return carry
 
-        lax.fori_loop(0, count, body, 0)
+        lax.fori_loop(0, count, body, 0, unroll=UNROLL)
 
     sweep(t_ref, buf_ref)
     sweep(buf_ref, o_ref)

time: 322 us -> 250 us (0.78)
  Pallas kernels: 151 us -> 67.2 us
  waiting for transfers between devices: 26.8 us -> 38.4 us
    pallas_call x2, Pallas kernels: 102 us -> 39.7 us  [run_thermal(): pl.pallas_call(kernel, out_shape=jax.ShapeDtypeStruct((n, w), jnp.float32...]
    pallas_call x2, Pallas kernels: 48.6 us -> 27.5 us  [run_power(): pl.pallas_call(power_kernel, out_shape=jax.ShapeDtypeStruct((n, w), jnp.f...]
    ppermute x7, waiting for transfers between devices: 25.5 us -> 37.1 us  [extended(): lax.ppermute(lax.slice_in_dim(block, 0, width, axis=dim), axis, backward)]
  transfers between devices with their start and end apart: 17 -> 17, of which waited for: 2 -> 2; matrix products, arithmetic and copies ran while one was open for 18% -> 24% of each run, Pallas kernels for 8% -> 6%
where the time goes in v2:
time: 250 us; the launch traced here: 246 us
  Pallas kernels  67.2 us (27%)
  local copies, waits for them, and re-layouts  55 us (22%)
  starting transfers between devices  50.3 us (20%)
  waiting for transfers between devices  38.4 us (15%)
  other arithmetic  32.7 us (13%)
    pallas_call x2, Pallas kernels, run_thermal(): pl.pallas_call(kernel, out_shape=jax.ShapeDtypeStruct((n, w), jnp.float32...  39.7 us
    ppermute x7, waiting for transfers between devices, extended(): lax.ppermute(lax.slice_in_dim(block, 0, width, axis=dim), axis, backward)  37.1 us
    pallas_call x2, Pallas kernels, run_power(): pl.pallas_call(power_kernel, out_shape=jax.ShapeDtypeStruct((n, w), jnp.f...  27.5 us
    ppermute x7, starting transfers between devices, extended(): lax.ppermute(lax.slice_in_dim(block, block.shape[dim] - width, None, axis...  24.9 us
    ppermute x7, starting transfers between devices, extended(): lax.ppermute(lax.slice_in_dim(block, 0, width, axis=dim), axis, backward)  13.9 us
    concatenate x3, local copies, waits for them, and re-layouts, extended(): block = jnp.concatenate([low, block, high], axis=dim)  11.6 us
    concatenate x4, other arithmetic, extended(): block = jnp.concatenate([low, block, high], axis=dim)  9.58 us
    all_to_all x2, starting transfers between devices, gather_heat(): lax.all_to_all(copies, 'col', split_axis=0, concat_axis=0, tiled=True)  7.81 us
  transfers between devices with their start and end apart: 17, of which 2 were waited for; matrix products, arithmetic and copies ran while one was open for 24% of the time, Pallas kernels for 6%

profile of v2, /device:TPU:8, one launch (start us, length us, event | category | flops | bytes accessed | tf_op | source)
XLA Modules:
  0.0 246.5 jit_solution(9090779495243774980)
XLA Ops:
  0.7 1.5 multiply_bitcast_fusion
  2.7 0.8 copy-done.14
  3.5 1.0 copy-done.20
  4.5 1.3 pad_maximum_fusion.6
  5.8 2.1 collective-permute-start.1
  7.9 2.4 collective-permute-start
  10.9 3.1 %collective-permute-start.4 = (s32[8,512]{1,0:T(8,128)S(1)}, s32[8,512]{1,0:T(8,128)S(1)}, u32[]{:S(2)}, u32[]{:S(2)}) collective-permute-start(s32[8,512]{1,0:T(8,128)S(1)} %get-tuple-element.24), channel_id=1, source_target_pairs={{0,4},{4,8},{8,12},{12,16},{16,20},{20,24},{24,28},{1,5},{5,9},{9,... | collective-permute-start | bytes 49160 | tf_op jit(solution)/shard_map/ppermute | solution.py:32
  14.1 2.5 collective-permute-start.11
  16.5 1.9 collective-permute-start.10
  19.1 0.7 fusion.19.rok_ref
  19.8 0.7 fusion.23.rok_ref
  20.5 0.8 pad_maximum_fusion.10
  22.5 1.1 reshape.293.rok_ref
  24.1 0.9 reshape.294.rok_ref
  26.2 3.6 %collective-permute-start.5 = (s32[8,512]{1,0:T(8,128)}, s32[8,512]{1,0:T(8,128)S(1)}, u32[]{:S(2)}, u32[]{:S(2)}) collective-permute-start(s32[8,512]{1,0:T(8,128)} %get-tuple-element.23), channel_id=1, source_target_pairs={{4,0},{8,4},{12,8},{16,12},{20,16},{24,20},{28,24},{5,1},{9,5},{13... | collective-permute-start | bytes 49160 | tf_op jit(solution)/shard_map/ppermute | solution.py:35
  29.9 1.9 collective-permute-start.7
  31.8 0.7 copy-done.25
  32.5 2.7 %collective-permute-start.6 = (f32[2,8,8,512]{3,2,1,0:T(8,128)}, f32[2,8,8,512]{3,2,1,0:T(8,128)}, u32[]{:S(2)}, u32[]{:S(2)}) collective-permute-start(f32[2,8,8,512]{3,2,1,0:T(8,128)} %get-tuple-element.17), channel_id=1, source_target_pairs={{0,4},{4,8},{8,12},{12,16},{16,20},{20,24},{24,28},{1,5},{5,9},{9,... | collective-permute-start | bytes 786440 | tf_op jit(solution)/shard_map/ppermute | solution.py:32
  35.2 2.0 pad_maximum_fusion.2
  37.2 2.8 %pad_maximum_fusion.1 = f32[3,376,1024]{2,1,0:T(8,128)S(1)} fusion(f32[3,60,1024]{2,1,0:T(8,128)} %collective-permute-done.1, f32[1,256,1024]{2,1,0:T(8,128)S(1)} %copy-done.15, f32[1,256,1024]{2,1,0:T(8,128)S(1)} %copy-done.13, f32[1,256,1024]{2,1,0:T(8,128)S(1)} %bitcast.104, f32[3,60,1024]{2,1,0:T(8,128)} %collective-permute-done), kind=kLoop, calls=%fused_computation.1 | loop fusion | flops 4620288 | bytes 9240576 | tf_op jit(solution)/shard_map/concatenate | solution.py:36
  40.0 2.1 copy-done.1
  42.1 1.2 fusion.44
  43.3 2.0 copy.33
  45.3 4.1 %collective-permute-start.2 = (f32[3,376,64]{1,2,0:T(8,128)}, f32[3,376,64]{1,2,0:T(8,128)}, u32[]{:S(2)}, u32[]{:S(2)}) collective-permute-start(f32[3,376,64]{1,2,0:T(8,128)} %copy.33), channel_id=1, source_target_pairs={{0,1},{1,2},{2,3},{4,5},{5,6},{6,7},{8,9},{9,10},{10,11},{12,13},{... | collective-permute-start | bytes 866312 | tf_op jit(solution)/shard_map/ppermute | solution.py:32
  49.5 2.0 copy.34
  51.4 1.3 collective-permute-start.3
  52.8 2.5 %pad_maximum_fusion.3 = f32[2,8,48,512]{3,2,1,0:T(8,128)} fusion(f32[2,8,8,512]{3,2,1,0:T(8,128)S(1)} %collective-permute-done.7, f32[1,8,32,512]{3,2,1,0:T(8,128)S(1)} %bitcast.98, f32[1,8,32,512]{3,2,1,0:T(8,128)} %bitcast.100, f32[2,8,8,512]{3,2,1,0:T(8,128)} %collective-permute-done.6), kind=kLoop, calls=%fused_computation.11 | loop fusion | flops 1179648 | bytes 3145728 | tf_op jit(solution)/shard_map/concatenate | solution.py:36
  55.3 1.3 collective-permute-start.9
  56.6 6.3 %collective-permute-start.8 = (f32[2,8,48,512]{3,2,1,0:T(8,128)}, f32[2,8,48,512]{3,2,1,0:T(8,128)}, u32[]{:S(2)}, u32[]{:S(2)}) collective-permute-start(f32[2,8,48,512]{3,2,1,0:T(8,128)} %pad_maximum_fusion.3), channel_id=1, source_target_pairs={{0,1},{1,2},{2,3},{4,5},{5,6},{6,7},{8,9},{9,10},{10,11},{12,13},{... | collective-permute-start | bytes 4718600 | tf_op jit(solution)/shard_map/ppermute | solution.py:32
  62.9 0.9 fusion.45
  63.9 4.4 %collective-permute-start.12 = (f32[2,312,64]{2,1,0:T(8,128)}, f32[2,312,64]{2,1,0:T(8,128)}, u32[]{:S(2)}, u32[]{:S(2)}) collective-permute-start(f32[2,312,64]{2,1,0:T(8,128)} %get-tuple-element.14), channel_id=1, source_target_pairs={{0,1},{1,2},{2,3},{4,5},{5,6},{6,7},{8,9},{9,10},{10,11},{12,13},{... | collective-permute-start | bytes 479240 | tf_op jit(solution)/shard_map/ppermute | solution.py:32
  68.3 1.2 copy.35
  69.5 1.3 collective-permute-start.13
  70.8 1.2 copy.36
  72.0 6.9 %concatenate.22 = f32[3,376,1152]{2,1,0:T(8,128)} concatenate(f32[3,376,64]{2,1,0:T(8,128)S(1)} %copy.35, f32[3,376,1024]{2,1,0:T(8,128)} %copy-done.1, f32[3,376,64]{2,1,0:T(8,128)S(1)} %copy.36), dimensions={2} | concatenate | bytes 10395648 | tf_op jit(solution)/shard_map/concatenate | solution.py:36
  78.9 4.9 %slice_bitcast_fusion = (f32[376,1152]{1,0:T(8,128)}, f32[376,1152]{1,0:T(8,128)}, f32[376,1152]{1,0:T(8,128)}) fusion(f32[3,376,1152]{2,1,0:T(8,128)} %concatenate.22), kind=kLoop, calls=%fused_computation.8 | loop fusion | bytes 10395648 | tf_op jit(solution)/shard_map/squeeze | solution.py:265
  83.8 1.3 broadcast_in_dim.36.d_ref
  85.2 14.8 %shard_map.86 = f32[376,1152]{1,0:T(8,128)} custom-call(f32[376,1152]{1,0:T(8,128)} %broadcast_in_dim.36.d_ref, f32[376,1152]{1,0:T(8,128)} %get-tuple-element.4.c_ref, f32[376,1152]{1,0:T(8,128)} %get-tuple-element.3.l_ref, f32[376,1152]{1,0:T(8,128)} %get-tuple-element.2.v_ref, f32[376,1]{1,0:T(8,128)} %fusion.19.rok_ref, f32[1,1152]{1,0:T(1,128)} %and_convert_fusion.cok_ref), custom_call_target="tpu_custom_call" | custom-call | tf_op jit(solution)/shard_map/pallas_call | solution.py:129
  100.0 2.9 %fusion.3 = f32[46,1024]{1,0:T(8,128)S(1)} fusion(f32[376,1152]{1,0:T(8,128)S(1)} %copy-done.3, f32[376,1152]{1,0:T(8,128)S(1)} %copy-done.2, f32[376,1152]{1,0:T(8,128)} %shard_map.86), kind=kLoop, calls=%fused_computation.14 | loop fusion | flops 2213888 | bytes 4710400 | tf_op jit(solution)/shard_map/reduce_sum | solution.py:55
  104.0 4.5 %all-to-all-start = ((f32[4,46,128]{2,1,0:T(8,128)}), f32[4,46,128]{2,1,0:T(8,128)S(1)}, u32[]{:S(2)}, u32[]{:S(2)}) async-start(f32[4,46,128]{2,1,0:T(8,128)} %broadcast_in_dim.37), calls=%async_computation | async-start | bytes 196608 | tf_op jit(solution)/shard_map/all_to_all | solution.py:274
  108.5 37.1 %collective-permute-done.13 = f32[2,312,64]{2,1,0:T(8,128)} collective-permute-done((f32[2,312,64]{2,1,0:T(8,128)}, f32[2,312,64]{2,1,0:T(8,128)}, u32[]{:S(2)}, u32[]{:S(2)}) %collective-permute-start.13) | collective-permute-done | bytes 159776 | tf_op jit(solution)/shard_map/ppermute | solution.py:35
  145.6 4.7 %concatenate.27 = f32[2,312,1152]{2,1,0:T(8,128)} concatenate(f32[2,312,64]{2,1,0:T(8,128)} %collective-permute-done.12, f32[2,312,1024]{2,1,0:T(8,128)} %copy-done.4, f32[2,312,64]{2,1,0:T(8,128)} %collective-permute-done.13), dimensions={2} | concatenate | bytes 5750784 | tf_op jit(solution)/shard_map/concatenate | solution.py:36
  150.5 2.1 bitcast_select_fusion.s_ref
  152.6 2.3 pad_maximum_fusion
  154.9 3.5 %fusion.43 = (f32[1,24,48,512]{3,2,1,0:T(8,128)}, f32[1,24,48,512]{3,2,1,0:T(8,128)}) fusion(f32[2,24,48,512]{3,2,1,0:T(8,128)S(1)} %pad_maximum_fusion), kind=kLoop, calls=%fused_computation.108 | loop fusion | bytes 9437184 | tf_op jit(solution)/shard_map/slice | solution.py:289
  158.5 1.7 reshape.281.t_ref
  160.2 25.0 %shard_map.87 = f32[1152,512]{1,0:T(8,128)} custom-call(f32[1152,512]{1,0:T(8,128)} %reshape.281.t_ref, f32[1152,512]{1,0:T(8,128)} %bitcast_select_fusion.s_ref, f32[1152,512]{1,0:T(8,128)} %bitcast.91, f32[1152,512]{1,0:T(8,128)} %bitcast.90, f32[1152,1]{1,0:T(8,128)} %reshape.293.rok_ref), custom_call_target="tpu_custom_call" | custom-call | tf_op jit(solution)/shard_map/pallas_call | solution.py:214
  185.3 1.3 fusion.11
  186.7 0.7 pad_maximum_fusion.11
  187.4 3.7 %all-to-all-start.1 = ((f32[4,40,144]{2,1,0:T(8,128)}), f32[4,40,144]{2,1,0:T(8,128)S(1)}, u32[]{:S(2)}, u32[]{:S(2)}) async-start(f32[4,40,144]{2,1,0:T(8,128)} %pad_maximum_fusion.11), calls=%async_computation.1 | async-start | bytes 327680 | tf_op jit(solution)/shard_map/all_to_all | solution.py:303
  191.1 2.5 %slice_bitcast_fusion.3.v_ref = f32[312,1152]{1,0:T(8,128)} fusion(f32[3,376,1152]{2,1,0:T(8,128)} %concatenate.22), kind=kLoop, calls=%fused_computation.16 | loop fusion | bytes 2875392 | tf_op jit(solution)/shard_map/slice | solution.py:316
  193.6 1.3 slice.190.d_ref
  194.9 1.3 all-to-all-done.1
  197.0 2.9 %slice_divide_fusion.c_ref = f32[312,1152]{1,0:T(8,128)} fusion(f32[320,1152]{1,0:T(8,128)S(1)} %broadcast_bitcast_fusion.1, f32[3,376,1152]{2,1,0:T(8,128)} %concatenate.22), kind=kLoop, calls=%fused_computation.21 | loop fusion | flops 359424 | bytes 4313088 | tf_op jit(solution)/shard_map/div | solution.py:313
  199.9 1.5 fusion.4.l_ref
  201.4 12.7 %shard_map.88 = f32[312,1152]{1,0:T(8,128)} custom-call(f32[312,1152]{1,0:T(8,128)} %slice.190.d_ref, f32[312,1152]{1,0:T(8,128)} %slice_divide_fusion.c_ref, f32[312,1152]{1,0:T(8,128)} %fusion.4.l_ref, f32[312,1152]{1,0:T(8,128)} %slice_bitcast_fusion.3.v_ref, f32[312,1]{1,0:T(8,128)} %fusion.23.rok_ref, f32[1,1152]{1,0:T(1,128)} %and_convert_fusion.cok_ref), custom_call_target="tpu_custom_call" | custom-call | tf_op jit(solution)/shard_map/pallas_call | solution.py:129
  214.1 2.5 %fusion.8 = f32[38,1024]{1,0:T(8,128)S(1)} fusion(f32[312,1152]{1,0:T(8,128)S(1)} %copy-done.6, f32[312,1152]{1,0:T(8,128)S(1)} %copy-done.7, f32[312,1152]{1,0:T(8,128)} %shard_map.88), kind=kLoop, calls=%fused_computation.28 | loop fusion | flops 1828864 | bytes 3891200 | tf_op jit(solution)/shard_map/reduce_sum | solution.py:55
  217.7 3.3 %all-to-all-start.2 = ((f32[4,38,128]{2,1,0:T(8,128)}), f32[4,38,128]{2,1,0:T(8,128)S(1)}, u32[]{:S(2)}, u32[]{:S(2)}) async-start(f32[4,38,128]{2,1,0:T(8,128)} %broadcast_in_dim.43), calls=%async_computation.2 | async-start | bytes 163840 | tf_op jit(solution)/shard_map/all_to_all | solution.py:274
  221.0 4.1 %fusion.42 = (f32[1,16,40,512]{3,2,1,0:T(8,128)}, f32[1,16,40,512]{3,2,1,0:T(8,128)}) fusion(f32[2,24,48,512]{3,2,1,0:T(8,128)} %copy-done), kind=kLoop, calls=%fused_computation.107 | loop fusion | bytes 5242880 | tf_op jit(solution)/shard_map/slice | solution.py:289
  225.2 1.2 slice.209
  227.0 1.3 slice.208
  228.4 1.4 bitcast_select_fusion.1.s_ref
  229.8 14.7 %shard_map.89 = f32[640,512]{1,0:T(8,128)} custom-call(f32[640,512]{1,0:T(8,128)} %bitcast.96, f32[640,512]{1,0:T(8,128)} %bitcast_select_fusion.1.s_ref, f32[640,512]{1,0:T(8,128)} %bitcast.95, f32[640,512]{1,0:T(8,128)} %bitcast.94, f32[640,1]{1,0:T(8,128)} %reshape.294.rok_ref), custom_call_target="tpu_custom_call" | custom-call | tf_op jit(solution)/shard_map/pallas_call | solution.py:214
  244.5 1.9 slice.215
  (122 shorter events, 8.7 us)
Async XLA Ops:
  0.6 1.5 copy-start.10
  0.6 1.8 copy-start.11
  2.5 1.0 copy-start.14
  2.5 2.0 copy-start.20
  2.7 3.1 %copy-start.12 = (f32[1,256,1024]{2,1,0:T(8,128)}, f32[1,256,1024]{2,1,0:T(8,128)S(1)}, u32[]{:S(2)}) copy-start(f32[1,256,1024]{2,1,0:T(8,128)S(1)} %add_bitcast_fusion) | copy-start | bytes 3145732
  4.5 5.8 %copy-start.26 = (s32[32,512]{1,0:T(8,128)S(1)}, s32[32,512]{1,0:T(8,128)}, u32[]{:S(2)}) copy-start(s32[32,512]{1,0:T(8,128)} %param.11) | copy-start | bytes 196612
  5.8 14.7 %copy-start.17 = (f32[8,32,512]{2,1,0:T(8,128)S(1)}, f32[8,32,512]{2,1,0:T(8,128)}, u32[]{:S(2)}) copy-start(f32[8,32,512]{2,1,0:T(8,128)} %param.13) | copy-start | bytes 1572868
  5.8 14.7 %copy-start.18 = (f32[8,32,512]{2,1,0:T(8,128)S(1)}, f32[8,32,512]{2,1,0:T(8,128)}, u32[]{:S(2)}) copy-start(f32[8,32,512]{2,1,0:T(8,128)} %param.12) | copy-start | bytes 1572868
  5.8 31.3 %collective-permute-start.1 = (f32[3,60,1024]{2,1,0:T(8,128)}, f32[3,60,1024]{2,1,0:T(8,128)}, u32[]{:S(2)}, u32[]{:S(2)}) collective-permute-start(f32[3,60,1024]{2,1,0:T(8,128)} %get-tuple-element.12), channel_id=1, source_target_pairs={{4,0},{8,4},{12,8},{16,12},{20,16},{24,20},{28,24},{5,1},{9,5},{13... | collective-permute-start | bytes 2211848 | tf_op jit(solution)/shard_map/ppermute | solution.py:35
  7.9 29.3 %collective-permute-start = (f32[3,60,1024]{2,1,0:T(8,128)}, f32[3,60,1024]{2,1,0:T(8,128)}, u32[]{:S(2)}, u32[]{:S(2)}) collective-permute-start(f32[3,60,1024]{2,1,0:T(8,128)} %get-tuple-element.11), channel_id=1, source_target_pairs={{0,4},{4,8},{8,12},{12,16},{16,20},{20,24},{24,28},{1,5},{5,9},{9,... | collective-permute-start | bytes 2211848 | tf_op jit(solution)/shard_map/ppermute | solution.py:32
  10.9 15.3 %collective-permute-start.4 = (s32[8,512]{1,0:T(8,128)S(1)}, s32[8,512]{1,0:T(8,128)S(1)}, u32[]{:S(2)}, u32[]{:S(2)}) collective-permute-start(s32[8,512]{1,0:T(8,128)S(1)} %get-tuple-element.24), channel_id=1, source_target_pairs={{0,4},{4,8},{8,12},{12,16},{16,20},{20,24},{24,28},{1,5},{5,9},{9,... | collective-permute-start | bytes 49160 | tf_op jit(solution)/shard_map/ppermute | solution.py:32
  14.1 15.8 %collective-permute-start.11 = (f32[2,28,1024]{2,1,0:T(8,128)S(1)}, f32[2,28,1024]{2,1,0:T(8,128)S(1)}, u32[]{:S(2)}, u32[]{:S(2)}) collective-permute-start(f32[2,28,1024]{2,1,0:T(8,128)S(1)} %get-tuple-element.16), channel_id=1, source_target_pairs={{4,0},{8,4},{12,8},{16,12},{20,16},{24,20},{28,24},{5,1},{9,5},{13... | collective-permute-start | bytes 688136 | tf_op jit(solution)/shard_map/ppermute | solution.py:35
  16.5 15.3 %collective-permute-start.10 = (f32[2,28,1024]{2,1,0:T(8,128)S(1)}, f32[2,28,1024]{2,1,0:T(8,128)S(1)}, u32[]{:S(2)}, u32[]{:S(2)}) collective-permute-start(f32[2,28,1024]{2,1,0:T(8,128)S(1)} %get-tuple-element.15), channel_id=1, source_target_pairs={{0,4},{4,8},{8,12},{12,16},{16,20},{20,24},{24,28},{1,5},{5,9},{9,... | collective-permute-start | bytes 688136 | tf_op jit(solution)/shard_map/ppermute | solution.py:32
  26.2 82.3 %collective-permute-start.5 = (s32[8,512]{1,0:T(8,128)}, s32[8,512]{1,0:T(8,128)S(1)}, u32[]{:S(2)}, u32[]{:S(2)}) collective-permute-start(s32[8,512]{1,0:T(8,128)} %get-tuple-element.23), channel_id=1, source_target_pairs={{4,0},{8,4},{12,8},{16,12},{20,16},{24,20},{28,24},{5,1},{9,5},{13... | collective-permute-start | bytes 49160 | tf_op jit(solution)/shard_map/ppermute | solution.py:35
  29.8 2.0 copy-start.24
  29.9 22.9 %collective-permute-start.7 = (f32[2,8,8,512]{3,2,1,0:T(8,128)}, f32[2,8,8,512]{3,2,1,0:T(8,128)S(1)}, u32[]{:S(2)}, u32[]{:S(2)}) collective-permute-start(f32[2,8,8,512]{3,2,1,0:T(8,128)} %get-tuple-element.18), channel_id=1, source_target_pairs={{4,0},{8,4},{12,8},{16,12},{20,16},{24,20},{28,24},{5,1},{9,5},{13... | collective-permute-start | bytes 786440 | tf_op jit(solution)/shard_map/ppermute | solution.py:35
  31.8 0.7 copy-start.25
  32.5 4.7 %copy-start.13 = (f32[1,256,1024]{2,1,0:T(8,128)S(1)}, f32[1,256,1024]{2,1,0:T(8,128)}, u32[]{:S(2)}) copy-start(f32[1,256,1024]{2,1,0:T(8,128)} %copy-done.12) | copy-start | bytes 3145732
  32.5 4.7 %copy-start.15 = (f32[1,256,1024]{2,1,0:T(8,128)S(1)}, f32[1,256,1024]{2,1,0:T(8,128)}, u32[]{:S(2)}) copy-start(f32[1,256,1024]{2,1,0:T(8,128)} %copy-done.14) | copy-start | bytes 3145732
  32.5 4.7 %copy-start.21 = (f32[256,1024]{1,0:T(8,128)S(1)}, f32[256,1024]{1,0:T(8,128)}, u32[]{:S(2)}) copy-start(f32[256,1024]{1,0:T(8,128)} %param.9) | copy-start | bytes 3145732
  32.5 20.3 %collective-permute-start.6 = (f32[2,8,8,512]{3,2,1,0:T(8,128)}, f32[2,8,8,512]{3,2,1,0:T(8,128)}, u32[]{:S(2)}, u32[]{:S(2)}) collective-permute-start(f32[2,8,8,512]{3,2,1,0:T(8,128)} %get-tuple-element.17), channel_id=1, source_target_pairs={{0,4},{4,8},{8,12},{12,16},{16,20},{20,24},{24,28},{1,5},{5,9},{9,... | collective-permute-start | bytes 786440 | tf_op jit(solution)/shard_map/ppermute | solution.py:32
  37.1 25.8 %copy-start.4 = (f32[2,312,1024]{2,1,0:T(8,128)}, f32[2,312,1024]{2,1,0:T(8,128)S(1)}, u32[]{:S(2)}) copy-start(f32[2,312,1024]{2,1,0:T(8,128)S(1)} %pad_maximum_fusion.2) | copy-start | bytes 7667716
  40.0 2.2 copy-start.1
  45.3 18.5 %collective-permute-start.2 = (f32[3,376,64]{1,2,0:T(8,128)}, f32[3,376,64]{1,2,0:T(8,128)}, u32[]{:S(2)}, u32[]{:S(2)}) collective-permute-start(f32[3,376,64]{1,2,0:T(8,128)} %copy.33), channel_id=1, source_target_pairs={{0,1},{1,2},{2,3},{4,5},{5,6},{6,7},{8,9},{9,10},{10,11},{12,13},{... | collective-permute-start | bytes 866312 | tf_op jit(solution)/shard_map/ppermute | solution.py:32
  51.4 18.0 %collective-permute-start.3 = (f32[3,376,64]{1,2,0:T(8,128)}, f32[3,376,64]{1,2,0:T(8,128)}, u32[]{:S(2)}, u32[]{:S(2)}) collective-permute-start(f32[3,376,64]{1,2,0:T(8,128)} %copy.34), channel_id=1, source_target_pairs={{1,0},{2,1},{3,2},{5,4},{6,5},{7,6},{9,8},{10,9},{11,10},{13,12},{... | collective-permute-start | bytes 866312 | tf_op jit(solution)/shard_map/ppermute | solution.py:35
  52.7 2.5 %copy-start.22 = (f32[2,8,8,512]{3,2,1,0:T(8,128)}, f32[2,8,8,512]{3,2,1,0:T(8,128)S(1)}, u32[]{:S(2)}) copy-start(f32[2,8,8,512]{3,2,1,0:T(8,128)S(1)} %collective-permute-done.7) | copy-start | bytes 786436
  55.3 97.2 %collective-permute-start.9 = (f32[2,8,48,512]{3,2,1,0:T(8,128)}, f32[2,8,48,512]{3,2,1,0:T(8,128)}, u32[]{:S(2)}, u32[]{:S(2)}) collective-permute-start(f32[2,8,48,512]{3,2,1,0:T(8,128)} %pad_maximum_fusion.3), channel_id=1, source_target_pairs={{1,0},{2,1},{3,2},{5,4},{6,5},{7,6},{9,8},{10,9},{11,10},{13,12},{... | collective-permute-start | bytes 4718600 | tf_op jit(solution)/shard_map/ppermute | solution.py:35
  56.6 96.0 %collective-permute-start.8 = (f32[2,8,48,512]{3,2,1,0:T(8,128)}, f32[2,8,48,512]{3,2,1,0:T(8,128)}, u32[]{:S(2)}, u32[]{:S(2)}) collective-permute-start(f32[2,8,48,512]{3,2,1,0:T(8,128)} %pad_maximum_fusion.3), channel_id=1, source_target_pairs={{0,1},{1,2},{2,3},{4,5},{5,6},{6,7},{8,9},{9,10},{10,11},{12,13},{... | collective-permute-start | bytes 4718600 | tf_op jit(solution)/shard_map/ppermute | solution.py:32
  63.9 44.7 %collective-permute-start.12 = (f32[2,312,64]{2,1,0:T(8,128)}, f32[2,312,64]{2,1,0:T(8,128)}, u32[]{:S(2)}, u32[]{:S(2)}) collective-permute-start(f32[2,312,64]{2,1,0:T(8,128)} %get-tuple-element.14), channel_id=1, source_target_pairs={{0,1},{1,2},{2,3},{4,5},{5,6},{6,7},{8,9},{9,10},{10,11},{12,13},{... | collective-permute-start | bytes 479240 | tf_op jit(solution)/shard_map/ppermute | solution.py:32
  69.5 76.1 %collective-permute-start.13 = (f32[2,312,64]{2,1,0:T(8,128)}, f32[2,312,64]{2,1,0:T(8,128)}, u32[]{:S(2)}, u32[]{:S(2)}) collective-permute-start(f32[2,312,64]{2,1,0:T(8,128)} %get-tuple-element.13), channel_id=1, source_target_pairs={{1,0},{2,1},{3,2},{5,4},{6,5},{7,6},{9,8},{10,9},{11,10},{13,12},{... | collective-permute-start | bytes 479240 | tf_op jit(solution)/shard_map/ppermute | solution.py:35
  85.2 14.8 %copy-start.2 = (f32[376,1152]{1,0:T(8,128)S(1)}, f32[376,1152]{1,0:T(8,128)}, u32[]{:S(2)}) copy-start(f32[376,1152]{1,0:T(8,128)} %get-tuple-element.3.l_ref) | copy-start | bytes 5197828
  85.2 14.8 %copy-start.3 = (f32[376,1152]{1,0:T(8,128)S(1)}, f32[376,1152]{1,0:T(8,128)}, u32[]{:S(2)}) copy-start(f32[376,1152]{1,0:T(8,128)} %get-tuple-element.4.c_ref) | copy-start | bytes 5197828
  104.0 46.4 %all-to-all-start = ((f32[4,46,128]{2,1,0:T(8,128)}), f32[4,46,128]{2,1,0:T(8,128)S(1)}, u32[]{:S(2)}, u32[]{:S(2)}) async-start(f32[4,46,128]{2,1,0:T(8,128)} %broadcast_in_dim.37), calls=%async_computation | async-start | bytes 196608 | tf_op jit(solution)/shard_map/all_to_all | solution.py:274
  108.5 42.0 %copy-start.27 = (pred[1152]{0:T(1024)(128)(4,1)S(1)}, pred[1152]{0:T(1024)(128)(4,1)}, u32[]{:S(2)}) copy-start(pred[1152]{0:T(1024)(128)(4,1)} %and.184) | copy-start | bytes 3460
  150.4 2.2 copy-start.19
  150.4 2.1 copy-start.23
  154.9 3.6 %copy-start = (f32[2,24,48,512]{3,2,1,0:T(8,128)}, f32[2,24,48,512]{3,2,1,0:T(8,128)S(1)}, u32[]{:S(2)}) copy-start(f32[2,24,48,512]{3,2,1,0:T(8,128)S(1)} %pad_maximum_fusion) | copy-start | bytes 14155780
  160.2 25.0 %copy-start.29 = (s32[8]{0:T(128)S(1)}, s32[8]{0:T(128)}, u32[]{:S(2)}) copy-start(s32[8]{0:T(128)} %iota_add_fusion.4) | copy-start | bytes 100
  187.4 6.2 %copy-start.5 = (f32[376,1152]{1,0:T(8,128)S(1)}, f32[376,1152]{1,0:T(8,128)}, u32[]{:S(2)}) copy-start(f32[376,1152]{1,0:T(8,128)} %shard_map.86) | copy-start | bytes 5197828
  187.4 8.7 %all-to-all-start.1 = ((f32[4,40,144]{2,1,0:T(8,128)}), f32[4,40,144]{2,1,0:T(8,128)S(1)}, u32[]{:S(2)}, u32[]{:S(2)}) async-start(f32[4,40,144]{2,1,0:T(8,128)} %pad_maximum_fusion.11), calls=%async_computation.1 | async-start | bytes 327680 | tf_op jit(solution)/shard_map/all_to_all | solution.py:303
  197.0 3.0 %copy-start.8 = (f32[2,312,1152]{2,1,0:T(8,128)S(1)}, f32[2,312,1152]{2,1,0:T(8,128)}, u32[]{:S(2)}) copy-start(f32[2,312,1152]{2,1,0:T(8,128)} %concatenate.27) | copy-start | bytes 8626180
  201.4 12.7 %copy-start.6 = (f32[312,1152]{1,0:T(8,128)S(1)}, f32[312,1152]{1,0:T(8,128)}, u32[]{:S(2)}) copy-start(f32[312,1152]{1,0:T(8,128)} %slice_divide_fusion.c_ref) | copy-start | bytes 4313092
  201.4 12.7 %copy-start.7 = (f32[312,1152]{1,0:T(8,128)S(1)}, f32[312,1152]{1,0:T(8,128)}, u32[]{:S(2)}) copy-start(f32[312,1152]{1,0:T(8,128)} %fusion.4.l_ref) | copy-start | bytes 4313092
  217.7 10.6 %all-to-all-start.2 = ((f32[4,38,128]{2,1,0:T(8,128)}), f32[4,38,128]{2,1,0:T(8,128)S(1)}, u32[]{:S(2)}, u32[]{:S(2)}) async-start(f32[4,38,128]{2,1,0:T(8,128)} %broadcast_in_dim.43), calls=%async_computation.2 | async-start | bytes 163840 | tf_op jit(solution)/shard_map/all_to_all | solution.py:274
  221.0 4.1 %copy-start.16 = (f32[1152,512]{1,0:T(8,128)S(1)}, f32[1152,512]{1,0:T(8,128)}, u32[]{:S(2)}) copy-start(f32[1152,512]{1,0:T(8,128)} %shard_map.87) | copy-start | bytes 7077892
  225.2 1.8 copy-start.9
  227.0 1.4 copy-start.28
